TPU v7x, 32 devices: a whole 2x2x4 slice. The times are simulated.
32 devices in a mesh: leaf: 8 (over z, y), blk: 4 (over x, core).
Axes of the slice: x: 2, y: 2, z: 4, core: 2. Of those that a mesh axis runs over, the one named last changes fastest.
Arguments:
- parent_inverse: bfloat16 [8, 512, 512], P('leaf', None, 'blk'), as said below
- leaf_inverse: bfloat16 [112, 512, 512], P('leaf', 'blk'), as said below
- coupling: bfloat16 [112, 512, 512], P('leaf', 'blk'), may hold values from -0.25 to 0.25
- sensitivity: bfloat16 [112, 512, 512], P('leaf', 'blk'), may hold values from -0.25 to 0.25
- parent_of: int32 [112, 1], P('leaf'), may hold values from 0 to 7
- leaf_field: bfloat16 [112, 512], P('leaf'), may hold values from -6 to 6
- parent_field: bfloat16 [8, 512], P('leaf', 'blk'), may hold values from -6 to 6
Outputs:
- leaf_grad: float32 [112, 512], P('leaf', 'blk')
- coupling_grad: float32 [8, 512], P('leaf', 'blk')
Inputs may be any that keep to these rules, and one draw needn't show every extreme that they name: `parent_of`: every one of the 8 separator supernodes is the parent of at least one leaf. `parent_inverse`: lower triangular with a positive diagonal. `leaf_inverse`: lower triangular with a positive diagonal.
All inputs are finite; a program needn't handle non-finite values.
Results may differ from a plain program's by a relative error of at most 0.0006.
Values may be sent and summed in bfloat16 or wider, within the bound.
No kernel may reach another device: no remote copies, remote signals or barrier semaphores. Data moves between devices by JAX's collectives and lax.ppermute only.
A program may use at most 128 MiB of HBM per device.

v0:
```python
import jax
import jax.numpy as jnp
from jax import lax
from jax.sharding import PartitionSpec as P


def body(parent_inverse, leaf_inverse, coupling, sensitivity, parent_of, leaf_field, parent_field):
    count = coupling.shape[0]
    share = coupling.shape[1]
    width = coupling.shape[2]
    offset = lax.axis_index("blk") * share
    cov_rows = jnp.einsum(
        "pkr,pkc->prc",
        parent_inverse,
        lax.all_gather(parent_inverse, "blk", axis=2, tiled=True),
        preferred_element_type=jnp.float32,
    ).astype(jnp.bfloat16)
    parent_ids = parent_of[:, 0]
    initial = (
        jnp.zeros((count, share, width), jnp.bfloat16),
        jnp.zeros((count, share), jnp.bfloat16),
    )
    pieces = (
        lax.all_gather(cov_rows, "leaf", axis=0, tiled=True),
        lax.all_gather(parent_field, "leaf", axis=0, tiled=True),
    )
    number = pieces[0].shape[0]
    inside = (parent_ids >= 0) & (parent_ids < number)
    position = jnp.clip(parent_ids, 0, number - 1)
    taken_cov = jnp.take(pieces[0], position, axis=0)
    taken_field = jnp.take(pieces[1], position, axis=0)
    chosen_cov = jnp.where(inside[:, None, None], taken_cov, initial[0])
    chosen_field = jnp.where(inside[:, None], taken_field, initial[1])
    panel = coupling
    mixed = jnp.einsum(
        "lik,lkc->lic",
        panel,
        lax.all_gather(leaf_inverse, "blk", axis=1, tiled=True),
        preferred_element_type=jnp.float32,
    ).astype(jnp.bfloat16)
    cross = jnp.zeros((count, share, width), jnp.float32) - jnp.einsum(
        "lrk,lkc->lrc",
        chosen_cov,
        lax.all_gather(mixed, "blk", axis=1, tiled=True),
        preferred_element_type=jnp.float32,
    )
    cross_half = cross.astype(jnp.bfloat16)
    panel = coupling
    update = lax.psum_scatter(
        jnp.einsum("lik,lia->kla", panel, cross_half, preferred_element_type=jnp.float32),
        "blk",
        scatter_dimension=0,
        tiled=True,
    )
    factor = leaf_inverse.astype(jnp.float32)
    partial_diag = jnp.sum(factor * factor, 1) - jnp.einsum(
        "lka,kla->la", factor, update, precision=lax.Precision.HIGHEST
    )
    diagonal = lax.psum_scatter(partial_diag, "blk", scatter_dimension=1, tiled=True)
    value = lax.dynamic_slice_in_dim(leaf_field, offset, share, 1).astype(jnp.float32)
    leaf_grad = 0.5 * (diagonal - value * value)
    returned = jnp.sum(sensitivity.astype(jnp.float32) * cross, 2) - chosen_field.astype(
        jnp.float32
    ) * jnp.einsum("lab,lb->la", sensitivity, leaf_field, preferred_element_type=jnp.float32)
    parent_total = lax.axis_size("leaf")
    owners = (
        parent_ids[:, None] == lax.broadcasted_iota(jnp.int32, (count, parent_total), 1)
    ).astype(jnp.float32)
    spread = jnp.einsum("lp,la->pa", owners, returned, precision=lax.Precision.HIGHEST)
    coupling_grad = lax.psum_scatter(spread, "leaf", scatter_dimension=0, tiled=True)
    return (leaf_grad, coupling_grad)


def solution(mesh):
    in_specs = (
        P("leaf", None, "blk"),
        P("leaf", "blk", None),
        P("leaf", "blk", None),
        P("leaf", "blk", None),
        P("leaf", None),
        P("leaf", None),
        P("leaf", "blk"),
    )
    out_specs = (P("leaf", "blk"), P("leaf", "blk"))
    return jax.shard_map(body, mesh=mesh, in_specs=in_specs, out_specs=out_specs, check_vma=False)
```

profile of v0, /device:TPU:0, one launch (start us, length us, event | category | flops | bytes accessed | tf_op | source)
XLA Modules:
  0.0 319.3 jit_solution(10498825598781214529)
XLA Ops:
  7.2 0.7 all-gather.6.cloned.1.call-update
  8.2 8.6 %all_gather.15 = bf16[1,512,512]{2,1,0:T(8,128)(2,1)S(1)} all-gather(bf16[1,512,128]{2,1,0:T(8,128)(2,1)S(1)} %copy-done.2), channel_id=1, replica_groups=mesh['leaf'=8,'blk'=4] {'blk'}, dimensions={2}, use_global_device_ids=true | all-gather | bytes 655360 | tf_op jit(solution)/shard_map/all_gather | solution.py:15
  16.9 0.9 convolution_convert_fusion.1
  17.8 46.8 %all-gather.6.cloned.1.call-done = bf16[14,512,512]{2,1,0:T(8,128)(2,1)} async-done(((bf16[14,128,512]{2,1,0:T(8,128)(2,1)}), bf16[14,512,512]{2,1,0:T(8,128)(2,1)}) %all-gather.6.cloned.1.call-update) | async-done | bytes 7340048 | tf_op jit(solution)/shard_map/all_gather | solution.py:38
  64.7 5.5 %convolution_convert_fusion = bf16[14,128,512]{2,1,0:T(8,128)(2,1)} fusion(bf16[14,128,512]{2,1,0:T(8,128)(2,1)S(1)} %copy-done, bf16[14,512,512]{2,1,0:T(8,128)(2,1)} %all-gather.6.cloned.1.call-done), kind=kOutput, calls=%fused_computation.13 | convolution fusion | flops 940441600 | bytes 11010048 | tf_op jit(solution)/shard_map/lik,lkc->lic/dot_general | solution.py:35
  70.3 0.6 copy-done.5
  70.9 36.3 %all-gather.10.cloned.1.call-done = bf16[1024,512]{1,0:T(8,128)(2,1)} async-done(((bf16[128,512]{1,0:T(8,128)(2,1)}), bf16[1024,512]{1,0:T(8,128)(2,1)}) %all-gather.10.cloned.1.call-update) | async-done | bytes 1048592 | tf_op jit(solution)/shard_map/all_gather | solution.py:24
  107.2 3.2 gather_fusion
  110.4 49.5 %all-gather.8.cloned.1.call-done = bf16[14,512,512]{2,1,0:T(8,128)(2,1)} async-done(((bf16[14,128,512]{2,1,0:T(8,128)(2,1)}), bf16[14,512,512]{2,1,0:T(8,128)(2,1)}) %all-gather.8.cloned.1.call-update) | async-done | bytes 7340048 | tf_op jit(solution)/shard_map/all_gather | solution.py:44
  159.8 5.4 %multiply_reduce_fusion.1 = (f32[14,128]{1,0:T(8,128)S(1)}, f32[14,128,512]{2,1,0:T(8,128)S(1)}) fusion(bf16[14,128,512]{2,1,0:T(8,128)(2,1)} %param.10, bf16[14,512,512]{2,1,0:T(8,128)(2,1)} %all-gather.8.cloned.1.call-done, bf16[14,128,512]{2,1,0:T(8,128)(2,1)} %gather_fusion, pred[14]{0:T(512)(128)(4,1)S(1)} %get-tuple-element.3, ...), kind=kOutput, calls=%fused_computation.4 | convolution fusion | flops 945027328 | bytes 14687260 | tf_op jit(solution)/shard_map/lrk,lkc->lrc/dot_general | solution.py:41
  165.2 7.3 %convolution_bitcast_fusion = f32[512,14,512]{0,2,1:T(8,128)} fusion(bf16[14,128,512]{2,1,0:T(8,128)(2,1)S(1)} %copy-done, f32[14,128,512]{2,1,0:T(8,128)S(1)} %get-tuple-element.5), kind=kOutput, calls=%fused_computation.2 | convolution fusion | flops 941359104 | bytes 20185088 | tf_op jit(solution)/shard_map/lik,lia->kla/dot_general | solution.py:50
  173.2 20.5 %all-gather.1 = bf16[8,1,128]{2,1,0:T(2,128)(2,1)S(1)} all-gather(bf16[1,1,128]{2,1,0:T(2,128)(2,1)S(1)} %bitcast.40), channel_id=1, replica_groups=mesh['leaf'=8,'blk'=4] {'leaf'}, dimensions={0}, use_global_device_ids=true | all-gather | bytes 2304 | tf_op jit(solution)/shard_map/all_gather | solution.py:25
  193.7 0.6 gather_fusion.1
  194.3 0.6 dynamic-slice
  194.9 1.9 multiply_reduce_fusion.2
  196.8 0.6 fusion.10
  197.7 17.3 %all-reduce = f32[8,128]{1,0:T(8,128)S(1)} all-reduce(f32[8,128]{1,0:T(8,128)S(1)} %fusion.13), channel_id=5, replica_groups=mesh['leaf'=8,'blk'=4] {'leaf'}, use_global_device_ids=true, to_apply=%region_4.5.clone | all-reduce | flops 1024 | bytes 8192
  214.9 67.8 %reduce-scatter.3.cloned.1.call-done = f32[128,14,512]{0,2,1:T(8,128)} async-done(((f32[512,14,512]{0,2,1:T(8,128)}), f32[128,14,512]{0,2,1:T(8,128)}) %reduce-scatter.3.cloned.1.call-update) | async-done | bytes 3670032 | tf_op jit(solution)/shard_map/reduce_scatter | solution.py:49
  282.8 5.1 %copy.17 = f32[14,512,128]{1,2,0:T(8,128)} copy(f32[14,512,128]{2,1,0:T(8,128)} %bitcast.36) | data formatting | bytes 7340032
  287.9 3.2 %multiply_reduce_fusion = f32[14,512]{1,0:T(8,128)S(1)} fusion(f32[14,512,128]{1,2,0:T(8,128)} %copy.17, bf16[14,128,512]{2,1,0:T(8,128)(2,1)} %param.8), kind=kLoop, calls=%fused_computation.3 | loop fusion | flops 2745344 | bytes 5533696 | tf_op jit(solution)/shard_map/lka,kla->la/dot_general | solution.py:56
  291.1 0.6 sub.13
  291.8 1.2 constant_dynamic-slice_fusion
  293.0 18.5 %reduce-scatter.5.cloned.1.call-done = f32[14,128]{1,0:T(8,128)} async-done(((f32[14,512]{1,0:T(8,128)}), f32[14,128]{1,0:T(8,128)}) %reduce-scatter.5.cloned.1.call-update) | async-done | bytes 7184 | tf_op jit(solution)/shard_map/reduce_scatter | solution.py:59
  311.5 1.3 subtract_multiply_fusion
  (28 shorter events, 1.4 us)
Async XLA Ops:
  7.2 57.5 %copy-start = (bf16[14,128,512]{2,1,0:T(8,128)(2,1)S(1)}, bf16[14,128,512]{2,1,0:T(8,128)(2,1)}, u32[]{:S(2)}) copy-start(bf16[14,128,512]{2,1,0:T(8,128)(2,1)} %param.9) | copy-start | bytes 5505028
  7.2 1.0 copy-start.2
  7.2 57.5 %all-gather.6.cloned.1.call-start = ((), (), s32[]{:S(2)}) async-start(), calls=%async_computation.2 | async-start | bytes 9175040 | tf_op jit(solution)/shard_map/all_gather | solution.py:38
  7.9 99.3 %all-gather.10.cloned.1.call-start = ((), (), s32[]{:S(2)}) async-start(), calls=%async_computation.6 | async-start | bytes 1179648 | tf_op jit(solution)/shard_map/all_gather | solution.py:24
  17.8 142.0 %all-gather.8.cloned.1.call-start = ((), (), s32[]{:S(2)}) async-start(), calls=%async_computation.3 | async-start | bytes 9175040 | tf_op jit(solution)/shard_map/all_gather | solution.py:44
  70.2 0.7 copy-start.5
  70.2 212.6 %reduce-scatter.3.cloned.1.call-start = ((), (), s32[]{:S(2)}) async-start(), calls=%async_computation.4 | async-start | bytes 18350080 | tf_op jit(solution)/shard_map/reduce_scatter | solution.py:49
  172.6 0.7 copy-start.4
  172.6 21.7 %copy-start.6 = (u32[32]{0:T(128)S(1)}, u32[32]{0:T(128)}, u32[]{:S(2)}) copy-start(u32[32]{0:T(128)} %constant.58) | copy-start | bytes 388
  172.6 24.2 %copy-start.3 = (bf16[14,512]{1,0:T(8,128)(2,1)S(1)}, bf16[14,512]{1,0:T(8,128)(2,1)}, u32[]{:S(2)}) copy-start(bf16[14,512]{1,0:T(8,128)(2,1)} %param.12) | copy-start | bytes 43012
  172.6 138.9 %reduce-scatter.5.cloned.1.call-start = ((), (), s32[]{:S(2)}) async-start(), calls=%async_computation.5 | async-start | bytes 40960 | tf_op jit(solution)/shard_map/reduce_scatter | solution.py:59
  194.3 2.5 copy-start.1
Sparse Core Ops, SparseCore 0:
  9.6 55.0 all-gather.5
  66.8 40.3 all-gather.9
  108.8 51.0 all-gather.7
  172.7 110.0 reduce-scatter.2
  291.9 19.5 reduce-scatter.4
where the time goes:
time: 320 us; the launch traced here: 319 us
  waiting for transfers between devices  220 us (69%)
  blocking collectives  46.4 us (14%)
  matrix products  20 us (6%)
  between operations  13.9 us (4%)
  local copies, waits for them, and re-layouts  12 us (4%)
  other arithmetic  7.09 us (2%)
    reduce_scatter x1, waiting for transfers between devices, body(): lax.psum_scatter(jnp.einsum('lik,lia->kla', panel, cross_half, preferred_...  67.8 us
    all_gather x1, waiting for transfers between devices, body(): lax.all_gather(mixed, 'blk', axis=1, tiled=True)  49.5 us
    all_gather x1, waiting for transfers between devices, body(): lax.all_gather(leaf_inverse, 'blk', axis=1, tiled=True)  46.8 us
    all_gather x1, waiting for transfers between devices, body(): lax.all_gather(cov_rows, 'leaf', axis=0, tiled=True)  36.3 us
    all_gather x1, blocking collectives, body(): lax.all_gather(parent_field, 'leaf', axis=0, tiled=True)  20.5 us
    reduce_scatter x1, waiting for transfers between devices, body(): lax.psum_scatter(partial_diag, 'blk', scatter_dimension=1, tiled=True)  18.5 us
    unnamed x1, blocking collectives  17.3 us
    all_gather x1, blocking collectives, body(): lax.all_gather(parent_inverse, 'blk', axis=2, tiled=True)  8.63 us
  transfers between devices with their start and end apart: 5, of which 5 were waited for; matrix products, arithmetic and copies ran while one was open for 5% of the time, Pallas kernels for 0%

commit v1 on v0

v1 whole, which is shorter than its diff:
```python
import jax
import jax.numpy as jnp
from jax import lax
from jax.sharding import PartitionSpec as P


def body(parent_inverse, leaf_inverse, coupling, sensitivity, parent_of, leaf_field, parent_field):
    count, share, width = coupling.shape
    offset = lax.axis_index("blk") * share
    cov_rows = jnp.einsum(
        "pkr,pkc->prc",
        parent_inverse,
        lax.all_gather(parent_inverse, "blk", axis=2, tiled=True),
        preferred_element_type=jnp.float32,
    ).astype(jnp.bfloat16)
    field_row = jnp.pad(parent_field, ((0, 0), (0, width - share)))[:, None, :]
    packed = jnp.concatenate([cov_rows, field_row], axis=1)
    pieces = lax.all_gather(packed, "leaf", axis=0, tiled=True)
    number = pieces.shape[0]
    parent_ids = parent_of[:, 0]
    position = jnp.clip(parent_ids, 0, number - 1)
    taken = jnp.take(pieces, position, axis=0)
    chosen_cov = taken[:, :share, :]
    chosen_field = taken[:, share, :share]
    full_inverse = lax.all_gather(leaf_inverse, "blk", axis=1, tiled=True)
    product = jnp.einsum(
        "lik,lkc->lic", coupling, full_inverse, preferred_element_type=jnp.float32
    )
    mixed = product.astype(jnp.bfloat16)
    cross = -jnp.einsum(
        "lrk,lkc->lrc",
        chosen_cov,
        lax.all_gather(mixed, "blk", axis=1, tiled=True),
        preferred_element_type=jnp.float32,
    )
    cross_half = cross.astype(jnp.bfloat16)
    factor = leaf_inverse.astype(jnp.float32)
    partial_diag = jnp.sum(factor * factor, 1) - jnp.sum(
        cross_half.astype(jnp.float32) * product, 1
    )
    diagonal = lax.psum_scatter(partial_diag, "blk", scatter_dimension=1, tiled=True)
    value = lax.dynamic_slice_in_dim(leaf_field, offset, share, 1).astype(jnp.float32)
    leaf_grad = 0.5 * (diagonal - value * value)
    returned = jnp.sum(sensitivity.astype(jnp.float32) * cross, 2) - chosen_field.astype(
        jnp.float32
    ) * jnp.einsum("lab,lb->la", sensitivity, leaf_field, preferred_element_type=jnp.float32)
    parent_total = lax.axis_size("leaf")
    owners = (
        parent_ids[:, None] == lax.broadcasted_iota(jnp.int32, (count, parent_total), 1)
    ).astype(jnp.float32)
    spread = jnp.einsum("lp,la->pa", owners, returned, precision=lax.Precision.HIGHEST)
    coupling_grad = lax.psum_scatter(spread, "leaf", scatter_dimension=0, tiled=True)
    return (leaf_grad, coupling_grad)


def solution(mesh):
    in_specs = (
        P("leaf", None, "blk"),
        P("leaf", "blk", None),
        P("leaf", "blk", None),
        P("leaf", "blk", None),
        P("leaf", None),
        P("leaf", None),
        P("leaf", "blk"),
    )
    out_specs = (P("leaf", "blk"), P("leaf", "blk"))
    return jax.shard_map(body, mesh=mesh, in_specs=in_specs, out_specs=out_specs, check_vma=False)
```

time: 320 us -> 198 us (0.62)
  waiting for transfers between devices: 220 us -> 125 us
  blocking collectives: 46.4 us -> 30.2 us
  local copies, waits for them, and re-layouts: 12 us -> 6.98 us
  matrix products: 20 us -> 15.8 us
    reduce_scatter x1 -> x0, waiting for transfers between devices: 67.8 us -> none  [body(): lax.psum_scatter(jnp.einsum('lik,lia->kla', panel, cross_half, preferred_...]
    all_gather x1 -> x0, blocking collectives: 20.5 us -> none  [body(): lax.all_gather(parent_field, 'leaf', axis=0, tiled=True)]
    reduce_scatter x1, waiting for transfers between devices: 18.5 us -> 0.01 us  [body(): lax.psum_scatter(partial_diag, 'blk', scatter_dimension=1, tiled=True)]
    dot_general x2 -> x1, matrix products: 12.9 us -> 6.57 us  [body(): jnp.einsum('lik,lkc->lic', coupling, full_inverse, preferred_element_type...]
    all_gather x2, waiting for transfers between devices: 83.1 us -> 77.8 us  [the longest x1 46.2 us: body(): full_inverse = lax.all_gather(leaf_inverse, 'blk', axis=1, tiled=True)]
    unnamed x18 -> x14, local copies, waits for them, and re-layouts: 8.29 us -> 3.07 us
    unnamed x1, blocking collectives: 17.3 us -> 21.3 us
    all_gather x1, waiting for transfers between devices: 49.5 us -> 46 us  [body(): lax.all_gather(mixed, 'blk', axis=1, tiled=True)]
  transfers between devices with their start and end apart: 5 -> 4, of which waited for: 5 -> 3; matrix products, arithmetic and copies ran while one was open for 5% -> 10% of each run, Pallas kernels for 0% -> 0%
where the time goes in v1:
time: 198 us
  waiting for transfers between devices  125 us (63%)
  blocking collectives  30.2 us (15%)
  matrix products  15.8 us (8%)
  between operations  13.9 us (7%)
  local copies, waits for them, and re-layouts  6.98 us (4%)
  other arithmetic  6.32 us (3%)
    all_gather x1, waiting for transfers between devices, body(): full_inverse = lax.all_gather(leaf_inverse, 'blk', axis=1, tiled=True)  46.2 us
    all_gather x1, waiting for transfers between devices, body(): lax.all_gather(mixed, 'blk', axis=1, tiled=True)  46 us
    all_gather x1, waiting for transfers between devices, body(): pieces = lax.all_gather(packed, 'leaf', axis=0, tiled=True)  31.7 us
    unnamed x1, blocking collectives  21.3 us
    all_gather x1, blocking collectives, body(): lax.all_gather(parent_inverse, 'blk', axis=2, tiled=True)  8.85 us
    dot_general x1, matrix products, body(): jnp.einsum('lrk,lkc->lrc', chosen_cov, lax.all_gather(mixed, 'blk', axis=...  6.6 us
    dot_general x1, matrix products, body(): jnp.einsum('lik,lkc->lic', coupling, full_inverse, preferred_element_type...  6.57 us
  transfers between devices with their start and end apart: 4, of which 3 were waited for; matrix products, arithmetic and copies ran while one was open for 10% of the time, Pallas kernels for 0%

profile of v1, /device:TPU:0, one launch (start us, length us, event | category | flops | bytes accessed | tf_op | source)
XLA Modules:
  0.0 197.9 jit_solution(16531933602218626384)
XLA Ops:
  7.2 0.7 all-gather.6.cloned.1.call-update
  7.9 0.0 all-gather.4.cloned.1.call-start
  8.0 0.7 pad_bitcast_fusion
  8.6 8.8 %all_gather.12 = bf16[1,512,512]{2,1,0:T(8,128)(2,1)S(1)} all-gather(bf16[1,512,128]{2,1,0:T(8,128)(2,1)} %param.7), channel_id=1, replica_groups=mesh['leaf'=8,'blk'=4] {'blk'}, dimensions={2}, use_global_device_ids=true | all-gather | bytes 655360 | tf_op jit(solution)/shard_map/all_gather | solution.py:13
  17.5 0.3 fusion.2
  17.7 0.7 pad_maximum_fusion
  18.5 0.0 all-gather.8.cloned.1.call-start
  18.5 46.2 %all-gather.6.cloned.1.call-done = bf16[14,512,512]{2,1,0:T(8,128)(2,1)} async-done(((bf16[14,128,512]{2,1,0:T(8,128)(2,1)}), bf16[14,512,512]{2,1,0:T(8,128)(2,1)}) %all-gather.6.cloned.1.call-update) | async-done | bytes 7340048 | tf_op jit(solution)/shard_map/all_gather | solution.py:25
  64.7 6.6 %fusion.15 = (bf16[14,128,512]{2,1,0:T(8,128)(2,1)}, f32[14,128,512]{2,1,0:T(8,128)}) fusion(bf16[14,128,512]{2,1,0:T(8,128)(2,1)S(1)} %copy-done, bf16[14,512,512]{2,1,0:T(8,128)(2,1)} %all-gather.6.cloned.1.call-done), kind=kOutput, calls=%fused_computation.31 | convolution fusion | flops 940441600 | bytes 14680064 | tf_op jit(solution)/shard_map/lik,lkc->lic/dot_general | solution.py:26
  71.3 0.0 reduce-scatter.2.cloned.1.call-start
  71.4 0.6 dynamic-slice
  72.0 1.9 multiply_reduce_fusion.2
  73.9 2.1 %fusion.5 = f32[14,1,128]{2,1,0:T(1,128)S(1)} fusion(bf16[14,128,512]{2,1,0:T(8,128)(2,1)} %param.10, bf16[14,512,1]{1,0,2:T(8,128)(2,1)S(1)} %bitcast.31), kind=kOutput, calls=%fused_computation.13 | convolution fusion | flops 1835008 | bytes 1856512 | tf_op jit(solution)/shard_map/lab,lb->la/dot_general | solution.py:46
  76.0 31.7 %all-gather.4.cloned.1.call-done = bf16[8,129,512]{2,1,0:T(8,128)(2,1)} async-done(((bf16[1,129,512]{2,1,0:T(8,128)(2,1)}), bf16[8,129,512]{2,1,0:T(8,128)(2,1)}) %all-gather.4.cloned.1.call-update) | async-done | bytes 1056784 | tf_op jit(solution)/shard_map/all_gather | solution.py:18
  107.7 3.2 %gather_fusion = bf16[14,129,512]{2,1,0:T(8,128)(2,1)} fusion(bf16[8,129,512]{2,1,0:T(8,128)(2,1)} %all-gather.4.cloned.1.call-done, s32[1024]{0:T(1024)S(1)} %pad_clamp_fusion), kind=kCustom, calls=%fused_computation | custom fusion | bytes 3698744 | tf_op jit(solution)/shard_map/jit(_take)/gather | solution.py:22
  110.9 1.8 broadcast_select_fusion
  112.7 1.3 copy-done.1
  114.0 46.0 %all-gather.8.cloned.1.call-done = bf16[14,512,512]{2,1,0:T(8,128)(2,1)} async-done(((bf16[14,128,512]{2,1,0:T(8,128)(2,1)}), bf16[14,512,512]{2,1,0:T(8,128)(2,1)}) %all-gather.8.cloned.1.call-update) | async-done | bytes 7340048 | tf_op jit(solution)/shard_map/all_gather | solution.py:33
  160.0 6.6 %multiply_reduce_fusion = (f32[14,128]{1,0:T(8,128)S(1)}, f32[14,512]{1,0:T(8,128)S(1)}) fusion(bf16[14,128,512]{2,1,0:T(8,128)(2,1)} %param.10, f32[14,128,512]{2,1,0:T(8,128)} %get-tuple-element.5, bf16[14,512,512]{2,1,0:T(8,128)(2,1)} %all-gather.8.cloned.1.call-done, bf16[14,129,512]{2,1,0:T(8,128)(2,1)} %copy-done.1), kind=kOutput, calls=%fused_computation.1 | convolution fusion | flops 946855168 | bytes 14715904 | tf_op jit(solution)/shard_map/lrk,lkc->lrc/dot_general | solution.py:30
  166.6 0.6 sub.9
  167.3 0.3 fusion.8
  167.5 21.3 %all-reduce.1 = f32[8,128]{1,0:T(8,128)S(1)} all-reduce(f32[8,128]{1,0:T(8,128)S(1)} %fusion.8), channel_id=3, replica_groups=mesh['leaf'=8,'blk'=4] {'leaf'}, use_global_device_ids=true, to_apply=%region_4.5.clone | all-reduce | flops 1024 | bytes 8192
  188.9 1.2 constant_dynamic-slice_fusion
  190.0 1.3 subtract_multiply_fusion
  (20 shorter events, 0.2 us)
Async XLA Ops:
  7.2 57.5 %copy-start = (bf16[14,128,512]{2,1,0:T(8,128)(2,1)S(1)}, bf16[14,128,512]{2,1,0:T(8,128)(2,1)}, u32[]{:S(2)}) copy-start(bf16[14,128,512]{2,1,0:T(8,128)(2,1)} %param.9) | copy-start | bytes 5505028
  7.2 10.3 %copy-start.2 = (bf16[1,512,128]{2,1,0:T(8,128)(2,1)S(1)}, bf16[1,512,128]{2,1,0:T(8,128)(2,1)}, u32[]{:S(2)}) copy-start(bf16[1,512,128]{2,1,0:T(8,128)(2,1)} %param.7) | copy-start | bytes 393220
  7.2 57.5 %all-gather.6.cloned.1.call-start = ((), (), s32[]{:S(2)}) async-start(), calls=%async_computation.2 | async-start | bytes 9175040 | tf_op jit(solution)/shard_map/all_gather | solution.py:25
  7.9 99.7 %all-gather.4.cloned.1.call-start = ((), (), s32[]{:S(2)}) async-start(), calls=%async_computation.1 | async-start | bytes 1253376 | tf_op jit(solution)/shard_map/all_gather | solution.py:18
  18.5 52.9 %copy-start.5 = (u32[32]{0:T(128)S(1)}, u32[32]{0:T(128)}, u32[]{:S(2)}) copy-start(u32[32]{0:T(128)} %constant.43) | copy-start | bytes 388
  18.5 53.5 %copy-start.4 = (s32[14,1]{0,1:T(1,128)S(1)}, s32[14,1]{0,1:T(1,128)}, u32[]{:S(2)}) copy-start(s32[14,1]{0,1:T(1,128)} %param.11) | copy-start | bytes 172
  18.5 141.5 %all-gather.8.cloned.1.call-start = ((), (), s32[]{:S(2)}) async-start(), calls=%async_computation.3 | async-start | bytes 9175040 | tf_op jit(solution)/shard_map/all_gather | solution.py:33
  71.3 2.6 %copy-start.3 = (bf16[14,512]{1,0:T(8,128)(2,1)S(1)}, bf16[14,512]{1,0:T(8,128)(2,1)}, u32[]{:S(2)}) copy-start(bf16[14,512]{1,0:T(8,128)(2,1)} %param.12) | copy-start | bytes 43012
  71.3 118.7 %reduce-scatter.2.cloned.1.call-start = ((), (), s32[]{:S(2)}) async-start(), calls=%async_computation.4 | async-start | bytes 40960 | tf_op jit(solution)/shard_map/reduce_scatter | solution.py:41
  112.7 1.3 copy-start.1
Sparse Core Ops, SparseCore 0:
  9.6 55.0 all-gather.5
  66.9 40.7 all-gather.3
  109.2 50.7 all-gather.7
  167.4 19.5 reduce-scatter.1

commit v2 on v1

v2 whole, which is shorter than its diff:
```python
import jax
import jax.numpy as jnp
from jax import lax
from jax.sharding import PartitionSpec as P


def swap(x, axis, mask):
    size = lax.axis_size(axis)
    return lax.ppermute(x, axis, [(i, i ^ mask) for i in range(size)])


def gather_blocks(x, axis):
    far = swap(x, axis, 2)
    near = swap(jnp.stack([x, far]), axis, 1)
    return [x, near[0], far, near[1]]


def shift(x, axis, step):
    size = lax.axis_size(axis)
    return lax.ppermute(x, axis, [(i, (i + step) % size) for i in range(size)])


def body(parent_inverse, leaf_inverse, coupling, sensitivity, parent_of, leaf_field, parent_field):
    count, share, width = coupling.shape
    me_blk = lax.axis_index("blk")
    me_leaf = lax.axis_index("leaf")
    number = lax.axis_size("leaf")
    offset = me_blk * share

    full_inverse = gather_blocks(leaf_inverse, "blk")
    upper_blocks = gather_blocks(parent_inverse, "blk")
    upper = jnp.take(jnp.stack(upper_blocks), jnp.arange(4) ^ me_blk, axis=0)
    upper = jnp.concatenate([upper[t] for t in range(4)], axis=2)
    cov_rows = jnp.einsum(
        "pkr,pkc->prc", parent_inverse, upper, preferred_element_type=jnp.float32
    ).astype(jnp.bfloat16)
    field_row = jnp.pad(parent_field, ((0, 0), (0, width - share)))[:, None, :]
    packed = jnp.concatenate([cov_rows, field_row], axis=1)[0]
    pieces = jnp.stack([packed] + [shift(packed, "leaf", s) for s in range(1, number)])
    parent_ids = parent_of[:, 0]
    position = (me_leaf - jnp.clip(parent_ids, 0, number - 1)) % number
    taken = jnp.take(pieces, position, axis=0)
    chosen_cov = taken[:, :share, :]
    chosen_field = taken[:, share, :share]

    def by_blocks(left, blocks):
        total = None
        for t, block in enumerate(blocks):
            cols = lax.dynamic_slice_in_dim(left, (me_blk ^ t) * share, share, 2)
            part = jnp.einsum("lik,lkc->lic", cols, block, preferred_element_type=jnp.float32)
            total = part if total is None else total + part
        return total

    product = by_blocks(coupling, full_inverse)
    mixed = product.astype(jnp.bfloat16)
    cross = -by_blocks(chosen_cov, gather_blocks(mixed, "blk"))
    cross_half = cross.astype(jnp.bfloat16)
    factor = leaf_inverse.astype(jnp.float32)
    partial_diag = jnp.sum(factor * factor, 1) - jnp.sum(
        cross_half.astype(jnp.float32) * product, 1
    )
    half = width // 2
    mine = lax.dynamic_slice_in_dim(partial_diag, (me_blk >> 1) * half, half, 1)
    other = lax.dynamic_slice_in_dim(partial_diag, (1 - (me_blk >> 1)) * half, half, 1)
    mine = mine + swap(other, "blk", 2)
    quarter = lax.dynamic_slice_in_dim(mine, (me_blk & 1) * share, share, 1)
    rest = lax.dynamic_slice_in_dim(mine, (1 - (me_blk & 1)) * share, share, 1)
    diagonal = quarter + swap(rest, "blk", 1)
    value = lax.dynamic_slice_in_dim(leaf_field, offset, share, 1).astype(jnp.float32)
    leaf_grad = 0.5 * (diagonal - value * value)
    returned = jnp.sum(sensitivity.astype(jnp.float32) * cross, 2) - chosen_field.astype(
        jnp.float32
    ) * jnp.einsum("lab,lb->la", sensitivity, leaf_field, preferred_element_type=jnp.float32)
    owners = (
        parent_ids[:, None] == lax.broadcasted_iota(jnp.int32, (count, number), 1)
    ).astype(jnp.float32)
    spread = jnp.einsum("lp,la->pa", owners, returned, precision=lax.Precision.HIGHEST)
    coupling_grad = lax.dynamic_slice_in_dim(spread, me_leaf, 1, 0)
    for s in range(1, number):
        row = lax.dynamic_slice_in_dim(spread, (me_leaf + s) % number, 1, 0)
        coupling_grad = coupling_grad + shift(row, "leaf", s)
    return (leaf_grad, coupling_grad)


def solution(mesh):
    in_specs = (
        P("leaf", None, "blk"),
        P("leaf", "blk", None),
        P("leaf", "blk", None),
        P("leaf", "blk", None),
        P("leaf", None),
        P("leaf", None),
        P("leaf", "blk"),
    )
    out_specs = (P("leaf", "blk"), P("leaf", "blk"))
    return jax.shard_map(body, mesh=mesh, in_specs=in_specs, out_specs=out_specs, check_vma=False)
```

time: 198 us -> 179 us (0.904)
  blocking collectives: 30.2 us -> 0 us
  starting transfers between devices: 0.16 us -> 27 us
  waiting for transfers between devices: 125 us -> 111 us
  between operations: 13.9 us -> 1.12 us
  other arithmetic: 6.32 us -> 14 us
  matrix products: 15.8 us -> 20.5 us
  local copies, waits for them, and re-layouts: 6.98 us -> 4.82 us
    all_gather x3 -> x0, waiting for transfers between devices: 124 us -> none  [the longest x1 46.2 us: body(): full_inverse = lax.all_gather(leaf_inverse, 'blk', axis=1, tiled=True)]
    ppermute x0 -> x22, waiting for transfers between devices: none -> 111 us  [the longest x8 78.3 us: swap(): return lax.ppermute(x, axis, [(i, i ^ mask) for i in range(size)])]
    ppermute x0 -> x22, starting transfers between devices: none -> 27 us  [the longest x14 18.8 us: shift(): return lax.ppermute(x, axis, [(i, (i + step) % size) for i in range(size)])]
    unnamed x1 -> x0, blocking collectives: 21.3 us -> none
    all_gather x1 -> x0, blocking collectives: 8.85 us -> none  [body(): lax.all_gather(parent_inverse, 'blk', axis=2, tiled=True)]
    another operation x0 -> x4, other arithmetic: none -> 8.71 us  [the longest x3 8.64 us: gather_blocks(): near = swap(jnp.stack([x, far]), axis, 1)]
    dot_general x3 -> x9, matrix products: 13.4 us -> 18.2 us  [the longest x8 17.9 us: by_blocks(): jnp.einsum('lik,lkc->lic', cols, block, preferred_element_type=jnp.float32)]
  transfers between devices with their start and end apart: 4 -> 22, of which waited for: 3 -> 9; matrix products, arithmetic and copies ran while one was open for 10% -> 13% of each run, Pallas kernels for 0% -> 0%
where the time goes in v2:
time: 179 us
  waiting for transfers between devices  111 us (62%)
  starting transfers between devices  27 us (15%)
  matrix products  20.5 us (11%)
  other arithmetic  14 us (8%)
  local copies, waits for them, and re-layouts  4.82 us (3%)
    ppermute x8, waiting for transfers between devices, swap(): return lax.ppermute(x, axis, [(i, i ^ mask) for i in range(size)])  78.3 us
    ppermute x14, waiting for transfers between devices, shift(): return lax.ppermute(x, axis, [(i, (i + step) % size) for i in range(size)])  33 us
    ppermute x14, starting transfers between devices, shift(): return lax.ppermute(x, axis, [(i, (i + step) % size) for i in range(size)])  18.8 us
    dot_general x8, matrix products, by_blocks(): jnp.einsum('lik,lkc->lic', cols, block, preferred_element_type=jnp.float32)  17.9 us
    another operation x3, other arithmetic, gather_blocks(): near = swap(jnp.stack([x, far]), axis, 1)  8.64 us
    ppermute x8, starting transfers between devices, swap(): return lax.ppermute(x, axis, [(i, i ^ mask) for i in range(size)])  8.23 us
  transfers between devices with their start and end apart: 22, of which 9 were waited for; matrix products, arithmetic and copies ran while one was open for 13% of the time, Pallas kernels for 0%

profile of v2, /device:TPU:0, one launch (start us, length us, event | category | flops | bytes accessed | tf_op | source)
XLA Modules:
  0.0 178.7 jit_solution(11885275560486925277)
XLA Ops:
  0.6 3.0 %collective-permute-start.9 = (bf16[14,128,512]{2,1,0:T(8,128)(2,1)}, bf16[14,128,512]{2,1,0:T(8,128)(2,1)S(1)}, u32[]{:S(2)}, u32[]{:S(2)}) collective-permute-start(bf16[14,128,512]{2,1,0:T(8,128)(2,1)} %param.8), channel_id=1, source_target_pairs={{0,2},{1,3},{2,0},{3,1},{4,6},{5,7},{6,4},{7,5},{8,10},{9,11},{10,... | collective-permute-start | bytes 5505032 | tf_op jit(solution)/shard_map/ppermute | solution.py:9
  3.7 40.2 %collective-permute-done.9 = bf16[14,128,512]{2,1,0:T(8,128)(2,1)S(1)} collective-permute-done((bf16[14,128,512]{2,1,0:T(8,128)(2,1)}, bf16[14,128,512]{2,1,0:T(8,128)(2,1)S(1)}, u32[]{:S(2)}, u32[]{:S(2)}) %collective-permute-start.9) | collective-permute-done | bytes 1835040 | tf_op jit(solution)/shard_map/ppermute | solution.py:9
  43.9 4.3 %pad_maximum_fusion = bf16[2,14,128,512]{3,2,1,0:T(8,128)(2,1)} fusion(bf16[1,14,128,512]{3,2,1,0:T(8,128)(2,1)S(1)} %bitcast.95, bf16[1,14,128,512]{3,2,1,0:T(8,128)(2,1)} %bitcast.94), kind=kLoop, calls=%fused_computation.2 | loop fusion | flops 1835008 | bytes 7340032 | tf_op jit(solution)/shard_map/stack | solution.py:14
  50.0 2.0 %multiply_reduce_fusion.2 = f32[14,512]{1,0:T(8,128)S(1)} fusion(bf16[14,128,512]{2,1,0:T(8,128)(2,1)} %param.8), kind=kLoop, calls=%fused_computation.8 | loop fusion | flops 2745344 | bytes 1863680 | tf_op jit(solution)/shard_map/reduce_sum | solution.py:59
  54.9 2.1 %fusion.3 = f32[14,128,512]{2,1,0:T(8,128)S(1)} fusion(bf16[2,14,128,512]{3,2,1,0:T(8,128)(2,1)} %collective-permute-done.10, bf16[14,128,512]{2,1,0:T(8,128)(2,1)S(1)} %copy-done, s32[]{:T(128)S(6)} %select_n.138), kind=kOutput, calls=%fused_computation.17 | convolution fusion | flops 234881024 | bytes 5963780 | tf_op jit(solution)/shard_map/lik,lkc->lic/dot_general | solution.py:50
  57.1 4.9 %fusion.50 = (bf16[14,128,512]{2,1,0:T(8,128)(2,1)}, f32[14,128,512]{2,1,0:T(8,128)}) fusion(bf16[2,14,128,512]{3,2,1,0:T(8,128)(2,1)} %collective-permute-done.10, bf16[14,128,512]{2,1,0:T(8,128)(2,1)S(1)} %copy-done, s32[]{:T(128)S(6)} %select_n.140, f32[14,128,512]{2,1,0:T(8,128)S(1)} %fusion.16, f32[14,128,512]{2,1,0:T(8,128)S(1)} %fusion.19, ...), kind=kOutput, calls=%fused_computation.108 | convolution fusion | flops 238551040 | bytes 18808836 | tf_op jit(solution)/shard_map/lik,lkc->lic/dot_general | solution.py:50
  63.9 2.1 %fusion.26 = f32[14,1,128]{2,1,0:T(1,128)S(1)} fusion(bf16[14,128,512]{2,1,0:T(8,128)(2,1)} %param.10, bf16[14,512,1]{1,0,2:T(8,128)(2,1)S(1)} %bitcast.100), kind=kOutput, calls=%fused_computation.57 | convolution fusion | flops 1835008 | bytes 1856512 | tf_op jit(solution)/shard_map/lab,lb->la/dot_general | solution.py:73
  67.1 37.3 %collective-permute-done.11 = bf16[14,128,512]{2,1,0:T(8,128)(2,1)} collective-permute-done((bf16[14,128,512]{2,1,0:T(8,128)(2,1)}, bf16[14,128,512]{2,1,0:T(8,128)(2,1)}, u32[]{:S(2)}, u32[]{:S(2)}) %collective-permute-start.11) | collective-permute-done | bytes 1835040 | tf_op jit(solution)/shard_map/ppermute | solution.py:9
  104.4 4.3 %pad_maximum_fusion.1 = bf16[2,14,128,512]{3,2,1,0:T(8,128)(2,1)} fusion(bf16[1,14,128,512]{3,2,1,0:T(8,128)(2,1)} %bitcast.32, bf16[1,14,128,512]{3,2,1,0:T(8,128)(2,1)} %bitcast.31), kind=kLoop, calls=%fused_computation.3 | loop fusion | flops 1835008 | bytes 7340032 | tf_op jit(solution)/shard_map/stack | solution.py:14
  110.9 3.4 %collective-permute-start.8 = (bf16[129,512]{1,0:T(8,128)(2,1)S(1)}, bf16[129,512]{1,0:T(8,128)(2,1)S(1)}, u32[]{:S(2)}, u32[]{:S(2)}) collective-permute-start(bf16[129,512]{1,0:T(8,128)(2,1)S(1)} %get-tuple-element.11), channel_id=1, source_target_pairs={{0,28},{4,0},{8,4},{12,8},{16,12},{20,16},{24,20},{28,24},{1,29},{... | collective-permute-start | bytes 396296 | tf_op jit(solution)/shard_map/ppermute | solution.py:20
  116.0 2.4 %collective-permute-done.2 = bf16[129,512]{1,0:T(8,128)(2,1)S(1)} collective-permute-done((bf16[129,512]{1,0:T(8,128)(2,1)S(1)}, bf16[129,512]{1,0:T(8,128)(2,1)S(1)}, u32[]{:S(2)}, u32[]{:S(2)}) %collective-permute-start.2) | collective-permute-done | bytes 132128 | tf_op jit(solution)/shard_map/ppermute | solution.py:20
  118.7 10.2 %collective-permute-done.3 = bf16[129,512]{1,0:T(8,128)(2,1)S(1)} collective-permute-done((bf16[129,512]{1,0:T(8,128)(2,1)S(1)}, bf16[129,512]{1,0:T(8,128)(2,1)S(1)}, u32[]{:S(2)}, u32[]{:S(2)}) %collective-permute-start.3) | collective-permute-done | bytes 132128 | tf_op jit(solution)/shard_map/ppermute | solution.py:20
  128.9 9.8 %collective-permute-done.4 = bf16[129,512]{1,0:T(8,128)(2,1)S(1)} collective-permute-done((bf16[129,512]{1,0:T(8,128)(2,1)S(1)}, bf16[129,512]{1,0:T(8,128)(2,1)S(1)}, u32[]{:S(2)}, u32[]{:S(2)}) %collective-permute-start.4) | collective-permute-done | bytes 132128 | tf_op jit(solution)/shard_map/ppermute | solution.py:20
  138.7 1.9 %collective-permute-start.5 = (bf16[129,512]{1,0:T(8,128)(2,1)S(1)}, bf16[129,512]{1,0:T(8,128)(2,1)S(1)}, u32[]{:S(2)}, u32[]{:S(2)}) collective-permute-start(bf16[129,512]{1,0:T(8,128)(2,1)S(1)} %get-tuple-element.11), channel_id=1, source_target_pairs={{0,16},{4,20},{8,24},{12,28},{16,0},{20,4},{24,8},{28,12},{1,17},{... | collective-permute-start | bytes 396296 | tf_op jit(solution)/shard_map/ppermute | solution.py:20
  140.6 5.8 %collective-permute-done.5 = bf16[129,512]{1,0:T(8,128)(2,1)S(1)} collective-permute-done((bf16[129,512]{1,0:T(8,128)(2,1)S(1)}, bf16[129,512]{1,0:T(8,128)(2,1)S(1)}, u32[]{:S(2)}, u32[]{:S(2)}) %collective-permute-start.5) | collective-permute-done | bytes 132128 | tf_op jit(solution)/shard_map/ppermute | solution.py:20
  146.5 2.1 %gather_fusion.1 = bf16[14,129,512]{2,1,0:T(8,128)(2,1)} fusion(bf16[8,129,512]{2,1,0:T(8,128)(2,1)S(1)} %bitcast_dynamic-update-slice_fusion, s32[1024]{0:T(1024)S(1)} %pad_clamp_fusion), kind=kCustom, calls=%fused_computation.1 | custom fusion | bytes 3698744 | tf_op jit(solution)/shard_map/jit(_take)/gather | solution.py:42
  150.6 2.1 %fusion.21 = f32[14,128,512]{2,1,0:T(8,128)S(1)} fusion(bf16[14,128,512]{2,1,0:T(8,128)(2,1)} %get-tuple-element.20, bf16[14,128,512]{2,1,0:T(8,128)(2,1)S(1)} %slice.58, s32[]{:T(128)S(6)} %select_n.137), kind=kOutput, calls=%fused_computation.39 | convolution fusion | flops 234881024 | bytes 5963780 | tf_op jit(solution)/shard_map/lik,lkc->lic/dot_general | solution.py:50
  152.7 2.1 %fusion.12 = f32[14,128,512]{2,1,0:T(8,128)S(1)} fusion(bf16[14,128,512]{2,1,0:T(8,128)(2,1)} %collective-permute-done.11, bf16[14,128,512]{2,1,0:T(8,128)(2,1)S(1)} %slice.58, s32[]{:T(128)S(6)} %select_n.139), kind=kOutput, calls=%fused_computation.30 | convolution fusion | flops 234881024 | bytes 5963780 | tf_op jit(solution)/shard_map/lik,lkc->lic/dot_general | solution.py:50
  154.9 2.3 %fusion.1 = f32[14,128,512]{2,1,0:T(8,128)S(1)} fusion(bf16[2,14,128,512]{3,2,1,0:T(8,128)(2,1)} %collective-permute-done.12, bf16[14,128,512]{2,1,0:T(8,128)(2,1)S(1)} %slice.58, s32[]{:T(128)S(6)} %select_n.138), kind=kOutput, calls=%fused_computation.13 | convolution fusion | flops 234881024 | bytes 5963780 | tf_op jit(solution)/shard_map/lik,lkc->lic/dot_general | solution.py:50
  158.0 3.1 %multiply_reduce_fusion = (f32[14,128]{1,0:T(8,128)S(1)}, f32[14,512]{1,0:T(8,128)S(1)}) fusion(bf16[14,128,512]{2,1,0:T(8,128)(2,1)S(1)} %copy-done.3, f32[14,128,512]{2,1,0:T(8,128)S(1)} %copy-done.2, bf16[2,14,128,512]{3,2,1,0:T(8,128)(2,1)} %collective-permute-done.12, bf16[14,128,512]{2,1,0:T(8,128)(2,1)S(1)} %slice.58, s32[]{:T(128)S(6)} %select_n.140, ...), kind=kOutput, calls=%fused_computation.4 | convolution fusion | flops 244964608 | bytes 18844676 | tf_op jit(solution)/shard_map/lik,lkc->lic/dot_general | solution.py:50
  163.1 4.7 %collective-permute-start.21 = (f32[1,128]{1,0:T(1,128)S(1)}, f32[1,128]{1,0:T(1,128)S(1)}, u32[]{:S(2)}, u32[]{:S(2)}) collective-permute-start(f32[1,128]{1,0:T(1,128)S(1)} %get-tuple-element.14), channel_id=1, source_target_pairs={{0,28},{4,0},{8,4},{12,8},{16,12},{20,16},{24,20},{28,24},{1,29},{... | collective-permute-start | bytes 1544 | tf_op jit(solution)/shard_map/ppermute | solution.py:20
  167.8 2.9 %collective-permute-start.18 = (f32[1,128]{1,0:T(1,128)S(1)}, f32[1,128]{1,0:T(1,128)S(1)}, u32[]{:S(2)}, u32[]{:S(2)}) collective-permute-start(f32[1,128]{1,0:T(1,128)S(1)} %get-tuple-element.17), channel_id=1, source_target_pairs={{0,16},{4,20},{8,24},{12,28},{16,0},{20,4},{24,8},{28,12},{1,17},{... | collective-permute-start | bytes 1544 | tf_op jit(solution)/shard_map/ppermute | solution.py:20
  170.8 2.0 %collective-permute-start.16 = (f32[1,128]{1,0:T(1,128)S(1)}, f32[1,128]{1,0:T(1,128)S(1)}, u32[]{:S(2)}, u32[]{:S(2)}) collective-permute-start(f32[1,128]{1,0:T(1,128)S(1)} %get-tuple-element.19), channel_id=1, source_target_pairs={{0,8},{4,12},{8,16},{12,20},{16,24},{20,28},{24,0},{28,4},{1,9},{5... | collective-permute-start | bytes 1544 | tf_op jit(solution)/shard_map/ppermute | solution.py:20
  172.8 3.3 %collective-permute-done.17 = f32[1,128]{1,0:T(1,128)S(1)} collective-permute-done((f32[1,128]{1,0:T(1,128)S(1)}, f32[1,128]{1,0:T(1,128)S(1)}, u32[]{:S(2)}, u32[]{:S(2)}) %collective-permute-start.17) | collective-permute-done | bytes 544 | tf_op jit(solution)/shard_map/ppermute | solution.py:20
  (87 shorter events, 19.2 us)
Async XLA Ops:
  0.6 51.4 %copy-start = (bf16[14,128,512]{2,1,0:T(8,128)(2,1)S(1)}, bf16[14,128,512]{2,1,0:T(8,128)(2,1)}, u32[]{:S(2)}) copy-start(bf16[14,128,512]{2,1,0:T(8,128)(2,1)} %param.9) | copy-start | bytes 5505028
  0.6 43.3 %collective-permute-start.9 = (bf16[14,128,512]{2,1,0:T(8,128)(2,1)}, bf16[14,128,512]{2,1,0:T(8,128)(2,1)S(1)}, u32[]{:S(2)}, u32[]{:S(2)}) collective-permute-start(bf16[14,128,512]{2,1,0:T(8,128)(2,1)} %param.8), channel_id=1, source_target_pairs={{0,2},{1,3},{2,0},{3,1},{4,6},{5,7},{6,4},{7,5},{8,10},{9,11},{10,... | collective-permute-start | bytes 5505032 | tf_op jit(solution)/shard_map/ppermute | solution.py:9
  48.2 6.8 %collective-permute-start.10 = (bf16[2,14,128,512]{3,2,1,0:T(8,128)(2,1)}, bf16[2,14,128,512]{3,2,1,0:T(8,128)(2,1)}, u32[]{:S(2)}, u32[]{:S(2)}) collective-permute-start(bf16[2,14,128,512]{3,2,1,0:T(8,128)(2,1)} %pad_maximum_fusion), channel_id=1, source_target_pairs={{0,1},{1,0},{2,3},{3,2},{4,5},{5,4},{6,7},{7,6},{8,9},{9,8},{10,11... | collective-permute-start | bytes 11010056 | tf_op jit(solution)/shard_map/ppermute | solution.py:9
  48.2 15.6 %collective-permute-start = (bf16[1,512,128]{2,1,0:T(8,128)(2,1)S(1)}, bf16[1,512,128]{2,1,0:T(8,128)(2,1)S(1)}, u32[]{:S(2)}, u32[]{:S(2)}) collective-permute-start(bf16[1,512,128]{2,1,0:T(8,128)(2,1)S(1)} %copy-done.6), channel_id=1, source_target_pairs={{0,2},{1,3},{2,0},{3,1},{4,6},{5,7},{6,4},{7,5},{8,10},{9,11},{10,... | collective-permute-start | bytes 393224 | tf_op jit(solution)/shard_map/ppermute | solution.py:9
  57.1 6.8 %copy-start.7 = (bf16[14,512]{1,0:T(8,128)(2,1)S(1)}, bf16[14,512]{1,0:T(8,128)(2,1)}, u32[]{:S(2)}) copy-start(bf16[14,512]{1,0:T(8,128)(2,1)} %param.12) | copy-start | bytes 43012
  62.0 42.4 %collective-permute-start.11 = (bf16[14,128,512]{2,1,0:T(8,128)(2,1)}, bf16[14,128,512]{2,1,0:T(8,128)(2,1)}, u32[]{:S(2)}, u32[]{:S(2)}) collective-permute-start(bf16[14,128,512]{2,1,0:T(8,128)(2,1)} %get-tuple-element.20), channel_id=1, source_target_pairs={{0,2},{1,3},{2,0},{3,1},{4,6},{5,7},{6,4},{7,5},{8,10},{9,11},{10,... | collective-permute-start | bytes 5505032 | tf_op jit(solution)/shard_map/ppermute | solution.py:9
  63.8 2.2 %collective-permute-start.1 = (bf16[2,1,512,128]{3,2,1,0:T(8,128)(2,1)S(1)}, bf16[2,1,512,128]{3,2,1,0:T(8,128)(2,1)S(1)}, u32[]{:S(2)}, u32[]{:S(2)}) collective-permute-start(bf16[2,1,512,128]{3,2,1,0:T(8,128)(2,1)S(1)} %pad_maximum_fusion.2), channel_id=1, source_target_pairs={{0,1},{1,0},{2,3},{3,2},{4,5},{5,4},{6,7},{7,6},{8,9},{9,8},{10,11... | collective-permute-start | bytes 786440 | tf_op jit(solution)/shard_map/ppermute | solution.py:9
  108.7 46.2 %collective-permute-start.12 = (bf16[2,14,128,512]{3,2,1,0:T(8,128)(2,1)}, bf16[2,14,128,512]{3,2,1,0:T(8,128)(2,1)}, u32[]{:S(2)}, u32[]{:S(2)}) collective-permute-start(bf16[2,14,128,512]{3,2,1,0:T(8,128)(2,1)} %pad_maximum_fusion.1), channel_id=1, source_target_pairs={{0,1},{1,0},{2,3},{3,2},{4,5},{5,4},{6,7},{7,6},{8,9},{9,8},{10,11... | collective-permute-start | bytes 11010056 | tf_op jit(solution)/shard_map/ppermute | solution.py:9
  109.0 9.4 %collective-permute-start.2 = (bf16[129,512]{1,0:T(8,128)(2,1)S(1)}, bf16[129,512]{1,0:T(8,128)(2,1)S(1)}, u32[]{:S(2)}, u32[]{:S(2)}) collective-permute-start(bf16[129,512]{1,0:T(8,128)(2,1)S(1)} %get-tuple-element.11), channel_id=1, source_target_pairs={{0,4},{4,8},{8,12},{12,16},{16,20},{20,24},{24,28},{28,0},{1,5},{5... | collective-permute-start | bytes 396296 | tf_op jit(solution)/shard_map/ppermute | solution.py:20
  110.9 35.5 %collective-permute-start.8 = (bf16[129,512]{1,0:T(8,128)(2,1)S(1)}, bf16[129,512]{1,0:T(8,128)(2,1)S(1)}, u32[]{:S(2)}, u32[]{:S(2)}) collective-permute-start(bf16[129,512]{1,0:T(8,128)(2,1)S(1)} %get-tuple-element.11), channel_id=1, source_target_pairs={{0,28},{4,0},{8,4},{12,8},{16,12},{20,16},{24,20},{28,24},{1,29},{... | collective-permute-start | bytes 396296 | tf_op jit(solution)/shard_map/ppermute | solution.py:20
  114.3 32.1 %collective-permute-start.7 = (bf16[129,512]{1,0:T(8,128)(2,1)S(1)}, bf16[129,512]{1,0:T(8,128)(2,1)S(1)}, u32[]{:S(2)}, u32[]{:S(2)}) collective-permute-start(bf16[129,512]{1,0:T(8,128)(2,1)S(1)} %get-tuple-element.11), channel_id=1, source_target_pairs={{0,24},{4,28},{8,0},{12,4},{16,8},{20,12},{24,16},{28,20},{1,25},{... | collective-permute-start | bytes 396296 | tf_op jit(solution)/shard_map/ppermute | solution.py:20
  116.0 30.4 %collective-permute-start.6 = (bf16[129,512]{1,0:T(8,128)(2,1)S(1)}, bf16[129,512]{1,0:T(8,128)(2,1)S(1)}, u32[]{:S(2)}, u32[]{:S(2)}) collective-permute-start(bf16[129,512]{1,0:T(8,128)(2,1)S(1)} %get-tuple-element.11), channel_id=1, source_target_pairs={{0,20},{4,24},{8,28},{12,0},{16,4},{20,8},{24,12},{28,16},{1,21},{... | collective-permute-start | bytes 396296 | tf_op jit(solution)/shard_map/ppermute | solution.py:20
  118.4 10.5 %collective-permute-start.3 = (bf16[129,512]{1,0:T(8,128)(2,1)S(1)}, bf16[129,512]{1,0:T(8,128)(2,1)S(1)}, u32[]{:S(2)}, u32[]{:S(2)}) collective-permute-start(bf16[129,512]{1,0:T(8,128)(2,1)S(1)} %get-tuple-element.11), channel_id=1, source_target_pairs={{0,8},{4,12},{8,16},{12,20},{16,24},{20,28},{24,0},{28,4},{1,9},{5... | collective-permute-start | bytes 396296 | tf_op jit(solution)/shard_map/ppermute | solution.py:20
  128.9 9.8 %collective-permute-start.4 = (bf16[129,512]{1,0:T(8,128)(2,1)S(1)}, bf16[129,512]{1,0:T(8,128)(2,1)S(1)}, u32[]{:S(2)}, u32[]{:S(2)}) collective-permute-start(bf16[129,512]{1,0:T(8,128)(2,1)S(1)} %get-tuple-element.11), channel_id=1, source_target_pairs={{0,12},{4,16},{8,20},{12,24},{16,28},{20,0},{24,4},{28,8},{1,13},{... | collective-permute-start | bytes 396296 | tf_op jit(solution)/shard_map/ppermute | solution.py:20
  138.7 7.7 %collective-permute-start.5 = (bf16[129,512]{1,0:T(8,128)(2,1)S(1)}, bf16[129,512]{1,0:T(8,128)(2,1)S(1)}, u32[]{:S(2)}, u32[]{:S(2)}) collective-permute-start(bf16[129,512]{1,0:T(8,128)(2,1)S(1)} %get-tuple-element.11), channel_id=1, source_target_pairs={{0,16},{4,20},{8,24},{12,28},{16,0},{20,4},{24,8},{28,12},{1,17},{... | collective-permute-start | bytes 396296 | tf_op jit(solution)/shard_map/ppermute | solution.py:20
  161.2 6.6 %collective-permute-start.13 = (f32[14,256]{1,0:T(8,128)S(1)}, f32[14,256]{1,0:T(8,128)S(1)}, u32[]{:S(2)}, u32[]{:S(2)}) collective-permute-start(f32[14,256]{1,0:T(8,128)S(1)} %constant_dynamic-slice_fusion.10), channel_id=1, source_target_pairs={{0,2},{1,3},{2,0},{3,1},{4,6},{5,7},{6,4},{7,5},{8,10},{9,11},{10,... | collective-permute-start | bytes 43016 | tf_op jit(solution)/shard_map/ppermute | solution.py:9
  163.0 7.7 %collective-permute-start.15 = (f32[1,128]{1,0:T(1,128)S(1)}, f32[1,128]{1,0:T(1,128)S(1)}, u32[]{:S(2)}, u32[]{:S(2)}) collective-permute-start(f32[1,128]{1,0:T(1,128)S(1)} %get-tuple-element.13), channel_id=1, source_target_pairs={{0,4},{4,8},{8,12},{12,16},{16,20},{20,24},{24,28},{28,0},{1,5},{5... | collective-permute-start | bytes 1544 | tf_op jit(solution)/shard_map/ppermute | solution.py:20
  163.1 7.7 %collective-permute-start.21 = (f32[1,128]{1,0:T(1,128)S(1)}, f32[1,128]{1,0:T(1,128)S(1)}, u32[]{:S(2)}, u32[]{:S(2)}) collective-permute-start(f32[1,128]{1,0:T(1,128)S(1)} %get-tuple-element.14), channel_id=1, source_target_pairs={{0,28},{4,0},{8,4},{12,8},{16,12},{20,16},{24,20},{28,24},{1,29},{... | collective-permute-start | bytes 1544 | tf_op jit(solution)/shard_map/ppermute | solution.py:20
  167.8 5.0 %collective-permute-start.20 = (f32[1,128]{1,0:T(1,128)S(1)}, f32[1,128]{1,0:T(1,128)S(1)}, u32[]{:S(2)}, u32[]{:S(2)}) collective-permute-start(f32[1,128]{1,0:T(1,128)S(1)} %get-tuple-element.15), channel_id=1, source_target_pairs={{0,24},{4,28},{8,0},{12,4},{16,8},{20,12},{24,16},{28,20},{1,25},{... | collective-permute-start | bytes 1544 | tf_op jit(solution)/shard_map/ppermute | solution.py:20
  167.8 5.0 %collective-permute-start.19 = (f32[1,128]{1,0:T(1,128)S(1)}, f32[1,128]{1,0:T(1,128)S(1)}, u32[]{:S(2)}, u32[]{:S(2)}) collective-permute-start(f32[1,128]{1,0:T(1,128)S(1)} %get-tuple-element.16), channel_id=1, source_target_pairs={{0,20},{4,24},{8,28},{12,0},{16,4},{20,8},{24,12},{28,16},{1,21},{... | collective-permute-start | bytes 1544 | tf_op jit(solution)/shard_map/ppermute | solution.py:20
  167.8 5.0 %collective-permute-start.18 = (f32[1,128]{1,0:T(1,128)S(1)}, f32[1,128]{1,0:T(1,128)S(1)}, u32[]{:S(2)}, u32[]{:S(2)}) collective-permute-start(f32[1,128]{1,0:T(1,128)S(1)} %get-tuple-element.17), channel_id=1, source_target_pairs={{0,16},{4,20},{8,24},{12,28},{16,0},{20,4},{24,8},{28,12},{1,17},{... | collective-permute-start | bytes 1544 | tf_op jit(solution)/shard_map/ppermute | solution.py:20
  170.7 5.4 %collective-permute-start.17 = (f32[1,128]{1,0:T(1,128)S(1)}, f32[1,128]{1,0:T(1,128)S(1)}, u32[]{:S(2)}, u32[]{:S(2)}) collective-permute-start(f32[1,128]{1,0:T(1,128)S(1)} %get-tuple-element.18), channel_id=1, source_target_pairs={{0,12},{4,16},{8,20},{12,24},{16,28},{20,0},{24,4},{28,8},{1,13},{... | collective-permute-start | bytes 1544 | tf_op jit(solution)/shard_map/ppermute | solution.py:20
  170.8 6.8 %collective-permute-start.16 = (f32[1,128]{1,0:T(1,128)S(1)}, f32[1,128]{1,0:T(1,128)S(1)}, u32[]{:S(2)}, u32[]{:S(2)}) collective-permute-start(f32[1,128]{1,0:T(1,128)S(1)} %get-tuple-element.19), channel_id=1, source_target_pairs={{0,8},{4,12},{8,16},{12,20},{16,24},{20,28},{24,0},{28,4},{1,9},{5... | collective-permute-start | bytes 1544 | tf_op jit(solution)/shard_map/ppermute | solution.py:20
  172.8 5.3 %collective-permute-start.14 = (f32[14,128]{1,0:T(8,128)S(1)}, f32[14,128]{1,0:T(8,128)S(1)}, u32[]{:S(2)}, u32[]{:S(2)}) collective-permute-start(f32[14,128]{1,0:T(8,128)S(1)} %constant_dynamic-slice_fusion.9), channel_id=1, source_target_pairs={{0,1},{1,0},{2,3},{3,2},{4,5},{5,4},{6,7},{7,6},{8,9},{9,8},{10,11... | collective-permute-start | bytes 21512 | tf_op jit(solution)/shard_map/ppermute | solution.py:9
  (8 other events, 26.7 us)

commit v3 on v2

--- a/solution.py
+++ b/solution.py
@@ -27,8 +27,11 @@
     number = lax.axis_size("leaf")
     offset = me_blk * share
 
-    full_inverse = gather_blocks(leaf_inverse, "blk")
-    upper_blocks = gather_blocks(parent_inverse, "blk")
+    upper_far = swap(parent_inverse, "blk", 2)
+    local_inverse, upper_far = lax.optimization_barrier((leaf_inverse, upper_far))
+    inverse_far = swap(local_inverse, "blk", 2)
+    upper_near = swap(jnp.stack([parent_inverse, upper_far]), "blk", 1)
+    upper_blocks = [parent_inverse, upper_near[0], upper_far, upper_near[1]]
     upper = jnp.take(jnp.stack(upper_blocks), jnp.arange(4) ^ me_blk, axis=0)
     upper = jnp.concatenate([upper[t] for t in range(4)], axis=2)
     cov_rows = jnp.einsum(
@@ -37,6 +40,9 @@
     field_row = jnp.pad(parent_field, ((0, 0), (0, width - share)))[:, None, :]
     packed = jnp.concatenate([cov_rows, field_row], axis=1)[0]
     pieces = jnp.stack([packed] + [shift(packed, "leaf", s) for s in range(1, number)])
+    near_in, pieces = lax.optimization_barrier((jnp.stack([local_inverse, inverse_far]), pieces))
+    inverse_near = swap(near_in, "blk", 1)
+    full_inverse = [leaf_inverse, inverse_near[0], inverse_far, inverse_near[1]]
     parent_ids = parent_of[:, 0]
     position = (me_leaf - jnp.clip(parent_ids, 0, number - 1)) % number
     taken = jnp.take(pieces, position, axis=0)

time: 179 us -> 148 us (0.83)
  waiting for transfers between devices: 111 us -> 78.6 us
  local copies, waits for them, and re-layouts: 4.82 us -> 7.42 us
  matrix products: 20.5 us -> 18.4 us
    ppermute x8, waiting for transfers between devices: 78.3 us -> 46.9 us  [swap(): return lax.ppermute(x, axis, [(i, i ^ mask) for i in range(size)])]
    another operation x3 -> x1, other arithmetic: 8.64 us -> 2.44 us  [gather_blocks(): near = swap(jnp.stack([x, far]), axis, 1)]
    another operation x0 -> x2, other arithmetic: none -> 4.54 us  [the longest x1 3.61 us: body(): jnp.stack([local_inverse, inverse_far])]
    unnamed x26 -> x30, local copies, waits for them, and re-layouts: 1.82 us -> 3.75 us
  transfers between devices with their start and end apart: 22 -> 22, of which waited for: 9 -> 10; matrix products, arithmetic and copies ran while one was open for 13% -> 11% of each run, Pallas kernels for 0% -> 0%
where the time goes in v3:
time: 148 us
  waiting for transfers between devices  78.6 us (53%)
  starting transfers between devices  28.6 us (19%)
  matrix products  18.4 us (12%)
  other arithmetic  13.9 us (9%)
  local copies, waits for them, and re-layouts  7.42 us (5%)
    ppermute x8, waiting for transfers between devices, swap(): return lax.ppermute(x, axis, [(i, i ^ mask) for i in range(size)])  46.9 us
    ppermute x14, waiting for transfers between devices, shift(): return lax.ppermute(x, axis, [(i, (i + step) % size) for i in range(size)])  31.8 us
    ppermute x14, starting transfers between devices, shift(): return lax.ppermute(x, axis, [(i, (i + step) % size) for i in range(size)])  20.2 us
    dot_general x8, matrix products, by_blocks(): jnp.einsum('lik,lkc->lic', cols, block, preferred_element_type=jnp.float32)  17.3 us
    ppermute x8, starting transfers between devices, swap(): return lax.ppermute(x, axis, [(i, i ^ mask) for i in range(size)])  8.45 us
    unnamed x30, local copies, waits for them, and re-layouts  3.75 us
    another operation x1, other arithmetic, body(): jnp.stack([local_inverse, inverse_far])  3.61 us
  transfers between devices with their start and end apart: 22, of which 10 were waited for; matrix products, arithmetic and copies ran while one was open for 11% of the time, Pallas kernels for 0%

profile of v3, /device:TPU:0, one launch (start us, length us, event | category | flops | bytes accessed | tf_op | source)
XLA Modules:
  0.0 148.0 jit_solution(12691784489225551837)
XLA Ops:
  0.6 3.0 %collective-permute-start = (bf16[1,512,128]{2,1,0:T(8,128)(2,1)}, bf16[1,512,128]{2,1,0:T(8,128)(2,1)S(1)}, u32[]{:S(2)}, u32[]{:S(2)}) collective-permute-start(bf16[1,512,128]{2,1,0:T(8,128)(2,1)} %param.7), channel_id=1, source_target_pairs={{0,2},{1,3},{2,0},{3,1},{4,6},{5,7},{6,4},{7,5},{8,10},{9,11},{10,... | collective-permute-start | bytes 393224 | tf_op jit(solution)/shard_map/ppermute | solution.py:9
  4.4 3.0 %collective-permute-done = bf16[1,512,128]{2,1,0:T(8,128)(2,1)S(1)} collective-permute-done((bf16[1,512,128]{2,1,0:T(8,128)(2,1)}, bf16[1,512,128]{2,1,0:T(8,128)(2,1)S(1)}, u32[]{:S(2)}, u32[]{:S(2)}) %collective-permute-start) | collective-permute-done | bytes 131104 | tf_op jit(solution)/shard_map/ppermute | solution.py:9
  15.3 3.2 %collective-permute-start.9 = (bf16[129,512]{1,0:T(8,128)(2,1)S(1)}, bf16[129,512]{1,0:T(8,128)(2,1)S(1)}, u32[]{:S(2)}, u32[]{:S(2)}) collective-permute-start(bf16[129,512]{1,0:T(8,128)(2,1)S(1)} %get-tuple-element.19), channel_id=1, source_target_pairs={{0,28},{4,0},{8,4},{12,8},{16,12},{20,16},{24,20},{28,24},{1,29},{... | collective-permute-start | bytes 396296 | tf_op jit(solution)/shard_map/ppermute | solution.py:20
  20.3 2.8 %collective-permute-done.3 = bf16[129,512]{1,0:T(8,128)(2,1)S(1)} collective-permute-done((bf16[129,512]{1,0:T(8,128)(2,1)S(1)}, bf16[129,512]{1,0:T(8,128)(2,1)S(1)}, u32[]{:S(2)}, u32[]{:S(2)}) %collective-permute-start.3) | collective-permute-done | bytes 132128 | tf_op jit(solution)/shard_map/ppermute | solution.py:20
  23.1 9.8 %collective-permute-done.4 = bf16[129,512]{1,0:T(8,128)(2,1)S(1)} collective-permute-done((bf16[129,512]{1,0:T(8,128)(2,1)S(1)}, bf16[129,512]{1,0:T(8,128)(2,1)S(1)}, u32[]{:S(2)}, u32[]{:S(2)}) %collective-permute-start.4) | collective-permute-done | bytes 132128 | tf_op jit(solution)/shard_map/ppermute | solution.py:20
  32.9 9.8 %collective-permute-done.5 = bf16[129,512]{1,0:T(8,128)(2,1)S(1)} collective-permute-done((bf16[129,512]{1,0:T(8,128)(2,1)S(1)}, bf16[129,512]{1,0:T(8,128)(2,1)S(1)}, u32[]{:S(2)}, u32[]{:S(2)}) %collective-permute-start.5) | collective-permute-done | bytes 132128 | tf_op jit(solution)/shard_map/ppermute | solution.py:20
  42.7 2.2 %collective-permute-start.6 = (bf16[129,512]{1,0:T(8,128)(2,1)S(1)}, bf16[129,512]{1,0:T(8,128)(2,1)S(1)}, u32[]{:S(2)}, u32[]{:S(2)}) collective-permute-start(bf16[129,512]{1,0:T(8,128)(2,1)S(1)} %get-tuple-element.19), channel_id=1, source_target_pairs={{0,16},{4,20},{8,24},{12,28},{16,0},{20,4},{24,8},{28,12},{1,17},{... | collective-permute-start | bytes 396296 | tf_op jit(solution)/shard_map/ppermute | solution.py:20
  44.9 5.8 %collective-permute-done.6 = bf16[129,512]{1,0:T(8,128)(2,1)S(1)} collective-permute-done((bf16[129,512]{1,0:T(8,128)(2,1)S(1)}, bf16[129,512]{1,0:T(8,128)(2,1)S(1)}, u32[]{:S(2)}, u32[]{:S(2)}) %collective-permute-start.6) | collective-permute-done | bytes 132128 | tf_op jit(solution)/shard_map/ppermute | solution.py:20
  51.9 3.6 %pad_maximum_fusion = bf16[2,14,128,512]{3,2,1,0:T(8,128)(2,1)} fusion(bf16[1,14,128,512]{3,2,1,0:T(8,128)(2,1)} %bitcast.2, bf16[1,14,128,512]{3,2,1,0:T(8,128)(2,1)S(1)} %bitcast.94), kind=kLoop, calls=%fused_computation.2 | loop fusion | flops 1835008 | bytes 7340032 | tf_op jit(solution)/shard_map/stack | solution.py:43
  55.5 2.1 %fusion.19 = f32[14,128,512]{2,1,0:T(8,128)S(1)} fusion(bf16[14,128,512]{2,1,0:T(8,128)(2,1)} %param.8, bf16[14,128,512]{2,1,0:T(8,128)(2,1)S(1)} %copy-done, s32[]{:T(128)S(6)} %select_n.137), kind=kOutput, calls=%fused_computation.37 | convolution fusion | flops 234881024 | bytes 5963780 | tf_op jit(solution)/shard_map/lik,lkc->lic/dot_general | solution.py:56
  57.6 2.1 %fusion.16 = f32[14,128,512]{2,1,0:T(8,128)S(1)} fusion(bf16[14,128,512]{2,1,0:T(8,128)(2,1)} %collective-permute-done.1, bf16[14,128,512]{2,1,0:T(8,128)(2,1)S(1)} %copy-done, s32[]{:T(128)S(6)} %select_n.139), kind=kOutput, calls=%fused_computation.34 | convolution fusion | flops 234881024 | bytes 5963780 | tf_op jit(solution)/shard_map/lik,lkc->lic/dot_general | solution.py:56
  59.8 2.5 %collective-permute-done.10 = bf16[2,14,128,512]{3,2,1,0:T(8,128)(2,1)} collective-permute-done((bf16[2,14,128,512]{3,2,1,0:T(8,128)(2,1)}, bf16[2,14,128,512]{3,2,1,0:T(8,128)(2,1)}, u32[]{:S(2)}, u32[]{:S(2)}) %collective-permute-start.10) | collective-permute-done | bytes 3670048 | tf_op jit(solution)/shard_map/ppermute | solution.py:9
  62.2 2.1 %fusion.3 = f32[14,128,512]{2,1,0:T(8,128)S(1)} fusion(bf16[2,14,128,512]{3,2,1,0:T(8,128)(2,1)} %collective-permute-done.10, bf16[14,128,512]{2,1,0:T(8,128)(2,1)S(1)} %copy-done, s32[]{:T(128)S(6)} %select_n.138), kind=kOutput, calls=%fused_computation.17 | convolution fusion | flops 234881024 | bytes 5963780 | tf_op jit(solution)/shard_map/lik,lkc->lic/dot_general | solution.py:56
  64.4 4.2 %fusion.50 = (bf16[14,128,512]{2,1,0:T(8,128)(2,1)S(1)}, f32[14,128,512]{2,1,0:T(8,128)}) fusion(bf16[2,14,128,512]{3,2,1,0:T(8,128)(2,1)} %collective-permute-done.10, bf16[14,128,512]{2,1,0:T(8,128)(2,1)S(1)} %copy-done, s32[]{:T(128)S(6)} %select_n.140, f32[14,128,512]{2,1,0:T(8,128)S(1)} %fusion.16, f32[14,128,512]{2,1,0:T(8,128)S(1)} %fusion.19, ...), kind=kOutput, calls=%fused_computation.108 | convolution fusion | flops 238551040 | bytes 18808836 | tf_op jit(solution)/shard_map/lik,lkc->lic/dot_general | solution.py:56
  70.4 40.3 %collective-permute-done.11 = bf16[14,128,512]{2,1,0:T(8,128)(2,1)S(1)} collective-permute-done((bf16[14,128,512]{2,1,0:T(8,128)(2,1)S(1)}, bf16[14,128,512]{2,1,0:T(8,128)(2,1)S(1)}, u32[]{:S(2)}, u32[]{:S(2)}) %collective-permute-start.11) | collective-permute-done | bytes 1835040 | tf_op jit(solution)/shard_map/ppermute | solution.py:9
  110.7 2.4 %pad_maximum_fusion.1 = bf16[2,14,128,512]{3,2,1,0:T(8,128)(2,1)} fusion(bf16[1,14,128,512]{3,2,1,0:T(8,128)(2,1)S(1)} %bitcast.96, bf16[1,14,128,512]{3,2,1,0:T(8,128)(2,1)S(1)} %bitcast.95), kind=kLoop, calls=%fused_computation.3 | loop fusion | flops 1835008 | bytes 7340032 | tf_op jit(solution)/shard_map/stack | solution.py:14
  113.3 2.0 %multiply_reduce_fusion.2 = f32[14,512]{1,0:T(8,128)S(1)} fusion(bf16[14,128,512]{2,1,0:T(8,128)(2,1)} %param.8), kind=kLoop, calls=%fused_computation.8 | loop fusion | flops 2745344 | bytes 1863680 | tf_op jit(solution)/shard_map/reduce_sum | solution.py:65
  115.9 2.1 %gather_fusion.1 = bf16[14,129,512]{2,1,0:T(8,128)(2,1)} fusion(bf16[8,129,512]{2,1,0:T(8,128)(2,1)S(1)} %bitcast_dynamic-update-slice_fusion, s32[1024]{0:T(1024)S(1)} %get-tuple-element.30), kind=kCustom, calls=%fused_computation.1 | custom fusion | bytes 3698744 | tf_op jit(solution)/shard_map/jit(_take)/gather | solution.py:48
  123.4 2.3 %fusion.1 = f32[14,128,512]{2,1,0:T(8,128)S(1)} fusion(bf16[2,14,128,512]{3,2,1,0:T(8,128)(2,1)} %collective-permute-done.12, bf16[14,128,512]{2,1,0:T(8,128)(2,1)S(1)} %slice.58, s32[]{:T(128)S(6)} %select_n.138), kind=kOutput, calls=%fused_computation.13 | convolution fusion | flops 234881024 | bytes 5963780 | tf_op jit(solution)/shard_map/lik,lkc->lic/dot_general | solution.py:56
  126.6 3.2 %multiply_reduce_fusion = (f32[14,128]{1,0:T(8,128)S(1)}, f32[14,512]{1,0:T(8,128)S(1)}) fusion(bf16[14,128,512]{2,1,0:T(8,128)(2,1)S(1)} %copy-done.6, f32[14,128,512]{2,1,0:T(8,128)S(1)} %copy-done.4, bf16[2,14,128,512]{3,2,1,0:T(8,128)(2,1)} %collective-permute-done.12, bf16[14,128,512]{2,1,0:T(8,128)(2,1)S(1)} %slice.58, s32[]{:T(128)S(6)} %select_n.140, ...), kind=kOutput, calls=%fused_computation.4 | convolution fusion | flops 244964608 | bytes 18844676 | tf_op jit(solution)/shard_map/lik,lkc->lic/dot_general | solution.py:56
  133.4 3.2 %collective-permute-start.21 = (f32[1,128]{1,0:T(1,128)S(1)}, f32[1,128]{1,0:T(1,128)S(1)}, u32[]{:S(2)}, u32[]{:S(2)}) collective-permute-start(f32[1,128]{1,0:T(1,128)S(1)} %get-tuple-element.22), channel_id=1, source_target_pairs={{0,28},{4,0},{8,4},{12,8},{16,12},{20,16},{24,20},{28,24},{1,29},{... | collective-permute-start | bytes 1544 | tf_op jit(solution)/shard_map/ppermute | solution.py:20
  138.4 3.0 %collective-permute-start.18 = (f32[1,128]{1,0:T(1,128)S(1)}, f32[1,128]{1,0:T(1,128)S(1)}, u32[]{:S(2)}, u32[]{:S(2)}) collective-permute-start(f32[1,128]{1,0:T(1,128)S(1)} %get-tuple-element.25), channel_id=1, source_target_pairs={{0,16},{4,20},{8,24},{12,28},{16,0},{20,4},{24,8},{28,12},{1,17},{... | collective-permute-start | bytes 1544 | tf_op jit(solution)/shard_map/ppermute | solution.py:20
  141.5 1.8 %collective-permute-start.16 = (f32[1,128]{1,0:T(1,128)S(1)}, f32[1,128]{1,0:T(1,128)S(1)}, u32[]{:S(2)}, u32[]{:S(2)}) collective-permute-start(f32[1,128]{1,0:T(1,128)S(1)} %get-tuple-element.27), channel_id=1, source_target_pairs={{0,8},{4,12},{8,16},{12,20},{16,24},{20,28},{24,0},{28,4},{1,9},{5... | collective-permute-start | bytes 1544 | tf_op jit(solution)/shard_map/ppermute | solution.py:20
  143.3 3.5 %collective-permute-done.17 = f32[1,128]{1,0:T(1,128)S(1)} collective-permute-done((f32[1,128]{1,0:T(1,128)S(1)}, f32[1,128]{1,0:T(1,128)S(1)}, u32[]{:S(2)}, u32[]{:S(2)}) %collective-permute-start.17) | collective-permute-done | bytes 544 | tf_op jit(solution)/shard_map/ppermute | solution.py:20
  (90 shorter events, 26.8 us)
Async XLA Ops:
  0.6 54.9 %copy-start = (bf16[14,128,512]{2,1,0:T(8,128)(2,1)S(1)}, bf16[14,128,512]{2,1,0:T(8,128)(2,1)}, u32[]{:S(2)}) copy-start(bf16[14,128,512]{2,1,0:T(8,128)(2,1)} %param.9) | copy-start | bytes 5505028
  0.6 6.7 %collective-permute-start = (bf16[1,512,128]{2,1,0:T(8,128)(2,1)}, bf16[1,512,128]{2,1,0:T(8,128)(2,1)S(1)}, u32[]{:S(2)}, u32[]{:S(2)}) collective-permute-start(bf16[1,512,128]{2,1,0:T(8,128)(2,1)} %param.7), channel_id=1, source_target_pairs={{0,2},{1,3},{2,0},{3,1},{4,6},{5,7},{6,4},{7,5},{8,10},{9,11},{10,... | collective-permute-start | bytes 393224 | tf_op jit(solution)/shard_map/ppermute | solution.py:9
  8.3 2.6 %collective-permute-start.2 = (bf16[2,1,512,128]{3,2,1,0:T(8,128)(2,1)S(1)}, bf16[2,1,512,128]{3,2,1,0:T(8,128)(2,1)S(1)}, u32[]{:S(2)}, u32[]{:S(2)}) collective-permute-start(bf16[2,1,512,128]{3,2,1,0:T(8,128)(2,1)S(1)} %pad_maximum_fusion.2), channel_id=1, source_target_pairs={{0,1},{1,0},{2,3},{3,2},{4,5},{5,4},{6,7},{7,6},{8,9},{9,8},{10,11... | collective-permute-start | bytes 786440 | tf_op jit(solution)/shard_map/ppermute | solution.py:9
  9.1 42.8 %collective-permute-start.1 = (bf16[14,128,512]{2,1,0:T(8,128)(2,1)}, bf16[14,128,512]{2,1,0:T(8,128)(2,1)}, u32[]{:S(2)}, u32[]{:S(2)}) collective-permute-start(bf16[14,128,512]{2,1,0:T(8,128)(2,1)} %param.8), channel_id=1, source_target_pairs={{0,2},{1,3},{2,0},{3,1},{4,6},{5,7},{6,4},{7,5},{8,10},{9,11},{10,... | collective-permute-start | bytes 5505032 | tf_op jit(solution)/shard_map/ppermute | solution.py:9
  13.8 9.3 %collective-permute-start.3 = (bf16[129,512]{1,0:T(8,128)(2,1)S(1)}, bf16[129,512]{1,0:T(8,128)(2,1)S(1)}, u32[]{:S(2)}, u32[]{:S(2)}) collective-permute-start(bf16[129,512]{1,0:T(8,128)(2,1)S(1)} %get-tuple-element.19), channel_id=1, source_target_pairs={{0,4},{4,8},{8,12},{12,16},{16,20},{20,24},{24,28},{28,0},{1,5},{5... | collective-permute-start | bytes 396296 | tf_op jit(solution)/shard_map/ppermute | solution.py:20
  15.3 35.5 %collective-permute-start.9 = (bf16[129,512]{1,0:T(8,128)(2,1)S(1)}, bf16[129,512]{1,0:T(8,128)(2,1)S(1)}, u32[]{:S(2)}, u32[]{:S(2)}) collective-permute-start(bf16[129,512]{1,0:T(8,128)(2,1)S(1)} %get-tuple-element.19), channel_id=1, source_target_pairs={{0,28},{4,0},{8,4},{12,8},{16,12},{20,16},{24,20},{28,24},{1,29},{... | collective-permute-start | bytes 396296 | tf_op jit(solution)/shard_map/ppermute | solution.py:20
  18.5 32.2 %collective-permute-start.8 = (bf16[129,512]{1,0:T(8,128)(2,1)S(1)}, bf16[129,512]{1,0:T(8,128)(2,1)S(1)}, u32[]{:S(2)}, u32[]{:S(2)}) collective-permute-start(bf16[129,512]{1,0:T(8,128)(2,1)S(1)} %get-tuple-element.19), channel_id=1, source_target_pairs={{0,24},{4,28},{8,0},{12,4},{16,8},{20,12},{24,16},{28,20},{1,25},{... | collective-permute-start | bytes 396296 | tf_op jit(solution)/shard_map/ppermute | solution.py:20
  20.3 30.4 %collective-permute-start.7 = (bf16[129,512]{1,0:T(8,128)(2,1)S(1)}, bf16[129,512]{1,0:T(8,128)(2,1)S(1)}, u32[]{:S(2)}, u32[]{:S(2)}) collective-permute-start(bf16[129,512]{1,0:T(8,128)(2,1)S(1)} %get-tuple-element.19), channel_id=1, source_target_pairs={{0,20},{4,24},{8,28},{12,0},{16,4},{20,8},{24,12},{28,16},{1,21},{... | collective-permute-start | bytes 396296 | tf_op jit(solution)/shard_map/ppermute | solution.py:20
  23.1 9.8 %collective-permute-start.4 = (bf16[129,512]{1,0:T(8,128)(2,1)S(1)}, bf16[129,512]{1,0:T(8,128)(2,1)S(1)}, u32[]{:S(2)}, u32[]{:S(2)}) collective-permute-start(bf16[129,512]{1,0:T(8,128)(2,1)S(1)} %get-tuple-element.19), channel_id=1, source_target_pairs={{0,8},{4,12},{8,16},{12,20},{16,24},{20,28},{24,0},{28,4},{1,9},{5... | collective-permute-start | bytes 396296 | tf_op jit(solution)/shard_map/ppermute | solution.py:20
  32.9 9.8 %collective-permute-start.5 = (bf16[129,512]{1,0:T(8,128)(2,1)S(1)}, bf16[129,512]{1,0:T(8,128)(2,1)S(1)}, u32[]{:S(2)}, u32[]{:S(2)}) collective-permute-start(bf16[129,512]{1,0:T(8,128)(2,1)S(1)} %get-tuple-element.19), channel_id=1, source_target_pairs={{0,12},{4,16},{8,20},{12,24},{16,28},{20,0},{24,4},{28,8},{1,13},{... | collective-permute-start | bytes 396296 | tf_op jit(solution)/shard_map/ppermute | solution.py:20
  42.7 8.0 %collective-permute-start.6 = (bf16[129,512]{1,0:T(8,128)(2,1)S(1)}, bf16[129,512]{1,0:T(8,128)(2,1)S(1)}, u32[]{:S(2)}, u32[]{:S(2)}) collective-permute-start(bf16[129,512]{1,0:T(8,128)(2,1)S(1)} %get-tuple-element.19), channel_id=1, source_target_pairs={{0,16},{4,20},{8,24},{12,28},{16,0},{20,4},{24,8},{28,12},{1,17},{... | collective-permute-start | bytes 396296 | tf_op jit(solution)/shard_map/ppermute | solution.py:20
  55.5 6.8 %collective-permute-start.10 = (bf16[2,14,128,512]{3,2,1,0:T(8,128)(2,1)}, bf16[2,14,128,512]{3,2,1,0:T(8,128)(2,1)}, u32[]{:S(2)}, u32[]{:S(2)}) collective-permute-start(bf16[2,14,128,512]{3,2,1,0:T(8,128)(2,1)} %pad_maximum_fusion), channel_id=1, source_target_pairs={{0,1},{1,0},{2,3},{3,2},{4,5},{5,4},{6,7},{7,6},{8,9},{9,8},{10,11... | collective-permute-start | bytes 11010056 | tf_op jit(solution)/shard_map/ppermute | solution.py:9
  68.6 44.5 %copy-start.2 = (bf16[14,128,512]{2,1,0:T(8,128)(2,1)}, bf16[14,128,512]{2,1,0:T(8,128)(2,1)S(1)}, u32[]{:S(2)}) copy-start(bf16[14,128,512]{2,1,0:T(8,128)(2,1)S(1)} %get-tuple-element.28) | copy-start | bytes 5505028
  68.6 42.1 %collective-permute-start.11 = (bf16[14,128,512]{2,1,0:T(8,128)(2,1)S(1)}, bf16[14,128,512]{2,1,0:T(8,128)(2,1)S(1)}, u32[]{:S(2)}, u32[]{:S(2)}) collective-permute-start(bf16[14,128,512]{2,1,0:T(8,128)(2,1)S(1)} %get-tuple-element.28), channel_id=1, source_target_pairs={{0,2},{1,3},{2,0},{3,1},{4,6},{5,7},{6,4},{7,5},{8,10},{9,11},{10,... | collective-permute-start | bytes 5505032 | tf_op jit(solution)/shard_map/ppermute | solution.py:9
  113.1 10.3 %collective-permute-start.12 = (bf16[2,14,128,512]{3,2,1,0:T(8,128)(2,1)}, bf16[2,14,128,512]{3,2,1,0:T(8,128)(2,1)}, u32[]{:S(2)}, u32[]{:S(2)}) collective-permute-start(bf16[2,14,128,512]{3,2,1,0:T(8,128)(2,1)} %pad_maximum_fusion.1), channel_id=1, source_target_pairs={{0,1},{1,0},{2,3},{3,2},{4,5},{5,4},{6,7},{7,6},{8,9},{9,8},{10,11... | collective-permute-start | bytes 11010056 | tf_op jit(solution)/shard_map/ppermute | solution.py:9
  129.8 8.6 %collective-permute-start.13 = (f32[14,256]{1,0:T(8,128)S(1)}, f32[14,256]{1,0:T(8,128)S(1)}, u32[]{:S(2)}, u32[]{:S(2)}) collective-permute-start(f32[14,256]{1,0:T(8,128)S(1)} %constant_dynamic-slice_fusion.10), channel_id=1, source_target_pairs={{0,2},{1,3},{2,0},{3,1},{4,6},{5,7},{6,4},{7,5},{8,10},{9,11},{10,... | collective-permute-start | bytes 43016 | tf_op jit(solution)/shard_map/ppermute | solution.py:9
  131.8 9.6 %collective-permute-start.15 = (f32[1,128]{1,0:T(1,128)S(1)}, f32[1,128]{1,0:T(1,128)S(1)}, u32[]{:S(2)}, u32[]{:S(2)}) collective-permute-start(f32[1,128]{1,0:T(1,128)S(1)} %get-tuple-element.21), channel_id=1, source_target_pairs={{0,4},{4,8},{8,12},{12,16},{16,20},{20,24},{24,28},{28,0},{1,5},{5... | collective-permute-start | bytes 1544 | tf_op jit(solution)/shard_map/ppermute | solution.py:20
  133.4 8.1 %collective-permute-start.21 = (f32[1,128]{1,0:T(1,128)S(1)}, f32[1,128]{1,0:T(1,128)S(1)}, u32[]{:S(2)}, u32[]{:S(2)}) collective-permute-start(f32[1,128]{1,0:T(1,128)S(1)} %get-tuple-element.22), channel_id=1, source_target_pairs={{0,28},{4,0},{8,4},{12,8},{16,12},{20,16},{24,20},{28,24},{1,29},{... | collective-permute-start | bytes 1544 | tf_op jit(solution)/shard_map/ppermute | solution.py:20
  136.6 6.7 %collective-permute-start.20 = (f32[1,128]{1,0:T(1,128)S(1)}, f32[1,128]{1,0:T(1,128)S(1)}, u32[]{:S(2)}, u32[]{:S(2)}) collective-permute-start(f32[1,128]{1,0:T(1,128)S(1)} %get-tuple-element.23), channel_id=1, source_target_pairs={{0,24},{4,28},{8,0},{12,4},{16,8},{20,12},{24,16},{28,20},{1,25},{... | collective-permute-start | bytes 1544 | tf_op jit(solution)/shard_map/ppermute | solution.py:20
  138.4 4.9 %collective-permute-start.19 = (f32[1,128]{1,0:T(1,128)S(1)}, f32[1,128]{1,0:T(1,128)S(1)}, u32[]{:S(2)}, u32[]{:S(2)}) collective-permute-start(f32[1,128]{1,0:T(1,128)S(1)} %get-tuple-element.24), channel_id=1, source_target_pairs={{0,20},{4,24},{8,28},{12,0},{16,4},{20,8},{24,12},{28,16},{1,21},{... | collective-permute-start | bytes 1544 | tf_op jit(solution)/shard_map/ppermute | solution.py:20
  138.4 4.9 %collective-permute-start.18 = (f32[1,128]{1,0:T(1,128)S(1)}, f32[1,128]{1,0:T(1,128)S(1)}, u32[]{:S(2)}, u32[]{:S(2)}) collective-permute-start(f32[1,128]{1,0:T(1,128)S(1)} %get-tuple-element.25), channel_id=1, source_target_pairs={{0,16},{4,20},{8,24},{12,28},{16,0},{20,4},{24,8},{28,12},{1,17},{... | collective-permute-start | bytes 1544 | tf_op jit(solution)/shard_map/ppermute | solution.py:20
  141.4 5.4 %collective-permute-start.17 = (f32[1,128]{1,0:T(1,128)S(1)}, f32[1,128]{1,0:T(1,128)S(1)}, u32[]{:S(2)}, u32[]{:S(2)}) collective-permute-start(f32[1,128]{1,0:T(1,128)S(1)} %get-tuple-element.26), channel_id=1, source_target_pairs={{0,12},{4,16},{8,20},{12,24},{16,28},{20,0},{24,4},{28,8},{1,13},{... | collective-permute-start | bytes 1544 | tf_op jit(solution)/shard_map/ppermute | solution.py:20
  141.5 5.4 %collective-permute-start.16 = (f32[1,128]{1,0:T(1,128)S(1)}, f32[1,128]{1,0:T(1,128)S(1)}, u32[]{:S(2)}, u32[]{:S(2)}) collective-permute-start(f32[1,128]{1,0:T(1,128)S(1)} %get-tuple-element.27), channel_id=1, source_target_pairs={{0,8},{4,12},{8,16},{12,20},{16,24},{20,28},{24,0},{28,4},{1,9},{5... | collective-permute-start | bytes 1544 | tf_op jit(solution)/shard_map/ppermute | solution.py:20
  143.3 4.1 %collective-permute-start.14 = (f32[14,128]{1,0:T(8,128)S(1)}, f32[14,128]{1,0:T(8,128)S(1)}, u32[]{:S(2)}, u32[]{:S(2)}) collective-permute-start(f32[14,128]{1,0:T(8,128)S(1)} %constant_dynamic-slice_fusion.9), channel_id=1, source_target_pairs={{0,1},{1,0},{2,3},{3,2},{4,5},{5,4},{6,7},{7,6},{8,9},{9,8},{10,11... | collective-permute-start | bytes 21512 | tf_op jit(solution)/shard_map/ppermute | solution.py:9
  (10 other events, 59.7 us)

commit v4 on v2

--- a/solution.py
+++ b/solution.py
@@ -9,15 +9,40 @@
     return lax.ppermute(x, axis, [(i, i ^ mask) for i in range(size)])
 
 
-def gather_blocks(x, axis):
-    far = swap(x, axis, 2)
-    near = swap(jnp.stack([x, far]), axis, 1)
-    return [x, near[0], far, near[1]]
+def far(x):
+    return swap(x, "blk", 2)
+
+
+def near(x, far_x):
+    both = swap(jnp.stack([x, far_x]), "blk", 1)
+    return [x, both[0], far_x, both[1]]
 
 
 def shift(x, axis, step):
     size = lax.axis_size(axis)
     return lax.ppermute(x, axis, [(i, (i + step) % size) for i in range(size)])
+
+
+def tied(*values):
+    return lax.optimization_barrier(values)
+
+
+def reduce_to_owner(spread, me, number):
+    if number & (number - 1):
+        total = lax.dynamic_slice_in_dim(spread, me, 1, 0)
+        for s in range(1, number):
+            row = lax.dynamic_slice_in_dim(spread, (me + s) % number, 1, 0)
+            total = total + shift(row, "leaf", s)
+        return total
+    current = spread
+    mask = number // 2
+    while mask:
+        upper = (me & mask) // mask
+        keep = lax.dynamic_slice_in_dim(current, upper * mask, mask, 0)
+        give = lax.dynamic_slice_in_dim(current, (1 - upper) * mask, mask, 0)
+        current = keep + swap(give, "leaf", mask)
+        mask //= 2
+    return current
 
 
 def body(parent_inverse, leaf_inverse, coupling, sensitivity, parent_of, leaf_field, parent_field):
@@ -26,22 +51,8 @@
     me_leaf = lax.axis_index("leaf")
     number = lax.axis_size("leaf")
     offset = me_blk * share
-
-    full_inverse = gather_blocks(leaf_inverse, "blk")
-    upper_blocks = gather_blocks(parent_inverse, "blk")
-    upper = jnp.take(jnp.stack(upper_blocks), jnp.arange(4) ^ me_blk, axis=0)
-    upper = jnp.concatenate([upper[t] for t in range(4)], axis=2)
-    cov_rows = jnp.einsum(
-        "pkr,pkc->prc", parent_inverse, upper, preferred_element_type=jnp.float32
-    ).astype(jnp.bfloat16)
-    field_row = jnp.pad(parent_field, ((0, 0), (0, width - share)))[:, None, :]
-    packed = jnp.concatenate([cov_rows, field_row], axis=1)[0]
-    pieces = jnp.stack([packed] + [shift(packed, "leaf", s) for s in range(1, number)])
-    parent_ids = parent_of[:, 0]
-    position = (me_leaf - jnp.clip(parent_ids, 0, number - 1)) % number
-    taken = jnp.take(pieces, position, axis=0)
-    chosen_cov = taken[:, :share, :]
-    chosen_field = taken[:, share, :share]
+    half_count = count // 2
+    parts = [slice(0, half_count), slice(half_count, count)]
 
     def by_blocks(left, blocks):
         total = None
@@ -51,9 +62,40 @@
             total = part if total is None else total + part
         return total
 
-    product = by_blocks(coupling, full_inverse)
-    mixed = product.astype(jnp.bfloat16)
-    cross = -by_blocks(chosen_cov, gather_blocks(mixed, "blk"))
+    upper_far = far(parent_inverse)
+    inverse_a, upper_far = tied(leaf_inverse[parts[0]], upper_far)
+    inverse_far_a = far(inverse_a)
+    upper_blocks = near(parent_inverse, upper_far)
+    upper = jnp.take(jnp.stack(upper_blocks), jnp.arange(4) ^ me_blk, axis=0)
+    upper = jnp.concatenate([upper[t] for t in range(4)], axis=2)
+    cov_rows = jnp.einsum(
+        "pkr,pkc->prc", parent_inverse, upper, preferred_element_type=jnp.float32
+    ).astype(jnp.bfloat16)
+    field_row = jnp.pad(parent_field, ((0, 0), (0, width - share)))[:, None, :]
+    packed = jnp.concatenate([cov_rows, field_row], axis=1)[0]
+    pieces = jnp.stack([packed] + [shift(packed, "leaf", s) for s in range(1, number)])
+
+    inverse_b, inverse_far_a = tied(leaf_inverse[parts[1]], inverse_far_a)
+    inverse_far_b = far(inverse_b)
+    product_a = by_blocks(coupling[parts[0]], near(inverse_a, inverse_far_a))
+    mixed_a = product_a.astype(jnp.bfloat16)
+    mixed_a, inverse_far_b, pieces = tied(mixed_a, inverse_far_b, pieces)
+    mixed_far_a = far(mixed_a)
+    product_b = by_blocks(coupling[parts[1]], near(inverse_b, inverse_far_b))
+    mixed_b = product_b.astype(jnp.bfloat16)
+    mixed_b, mixed_far_a = tied(mixed_b, mixed_far_a)
+    mixed_far_b = far(mixed_b)
+
+    parent_ids = parent_of[:, 0]
+    position = (me_leaf - jnp.clip(parent_ids, 0, number - 1)) % number
+    taken = jnp.take(pieces, position, axis=0)
+    chosen_cov = taken[:, :share, :]
+    chosen_field = taken[:, share, :share]
+
+    cross_a = -by_blocks(chosen_cov[parts[0]], near(mixed_a, mixed_far_a))
+    cross_b = -by_blocks(chosen_cov[parts[1]], near(mixed_b, mixed_far_b))
+    cross = jnp.concatenate([cross_a, cross_b], axis=0)
+    product = jnp.concatenate([product_a, product_b], axis=0)
     cross_half = cross.astype(jnp.bfloat16)
     factor = leaf_inverse.astype(jnp.float32)
     partial_diag = jnp.sum(factor * factor, 1) - jnp.sum(
@@ -75,10 +117,7 @@
         parent_ids[:, None] == lax.broadcasted_iota(jnp.int32, (count, number), 1)
     ).astype(jnp.float32)
     spread = jnp.einsum("lp,la->pa", owners, returned, precision=lax.Precision.HIGHEST)
-    coupling_grad = lax.dynamic_slice_in_dim(spread, me_leaf, 1, 0)
-    for s in range(1, number):
-        row = lax.dynamic_slice_in_dim(spread, (me_leaf + s) % number, 1, 0)
-        coupling_grad = coupling_grad + shift(row, "leaf", s)
+    coupling_grad = reduce_to_owner(spread, me_leaf, number)
     return (leaf_grad, coupling_grad)
 
 

time: 179 us -> 140 us (0.78)
  waiting for transfers between devices: 111 us -> 71.9 us
  local copies, waits for them, and re-layouts: 4.82 us -> 10.5 us
  other arithmetic: 14 us -> 8.9 us
  matrix products: 20.5 us -> 17.7 us
  starting transfers between devices: 27 us -> 29.7 us
    ppermute x14 -> x7, waiting for transfers between devices: 33 us -> 6.01 us  [shift(): return lax.ppermute(x, axis, [(i, (i + step) % size) for i in range(size)])]
    ppermute x8 -> x15, waiting for transfers between devices: 78.3 us -> 65.9 us  [swap(): return lax.ppermute(x, axis, [(i, i ^ mask) for i in range(size)])]
    ppermute x8 -> x15, starting transfers between devices: 8.23 us -> 17.2 us  [swap(): return lax.ppermute(x, axis, [(i, i ^ mask) for i in range(size)])]
    ppermute x14 -> x7, starting transfers between devices: 18.8 us -> 12.4 us  [shift(): return lax.ppermute(x, axis, [(i, (i + step) % size) for i in range(size)])]
    slice x2 -> x4, local copies, waits for them, and re-layouts: 0.2 us -> 4.42 us  [the longest x1 2.6 us: body(): product_b = by_blocks(coupling[parts[1]], near(inverse_b, inverse_far_b))]
    another operation x3 -> x5, other arithmetic: 8.64 us -> 4.41 us  [near(): both = swap(jnp.stack([x, far_x]), 'blk', 1)]
    dot_general x8 -> x16, matrix products: 17.9 us -> 15 us  [by_blocks(): jnp.einsum('lik,lkc->lic', cols, block, preferred_element_type=jnp.float32)]
  transfers between devices with their start and end apart: 22 -> 22, of which waited for: 9 -> 10; matrix products, arithmetic and copies ran while one was open for 13% -> 21% of each run, Pallas kernels for 0% -> 0%
where the time goes in v4:
time: 140 us
  waiting for transfers between devices  71.9 us (51%)
  starting transfers between devices  29.7 us (21%)
  matrix products  17.7 us (13%)
  local copies, waits for them, and re-layouts  10.5 us (8%)
  other arithmetic  8.9 us (6%)
    ppermute x15, waiting for transfers between devices, swap(): return lax.ppermute(x, axis, [(i, i ^ mask) for i in range(size)])  65.9 us
    ppermute x15, starting transfers between devices, swap(): return lax.ppermute(x, axis, [(i, i ^ mask) for i in range(size)])  17.2 us
    dot_general x16, matrix products, by_blocks(): jnp.einsum('lik,lkc->lic', cols, block, preferred_element_type=jnp.float32)  15 us
    ppermute x7, starting transfers between devices, shift(): return lax.ppermute(x, axis, [(i, (i + step) % size) for i in range(size)])  12.4 us
    ppermute x7, waiting for transfers between devices, shift(): return lax.ppermute(x, axis, [(i, (i + step) % size) for i in range(size)])  6.01 us
    another operation x5, other arithmetic, near(): both = swap(jnp.stack([x, far_x]), 'blk', 1)  4.41 us
    unnamed x38, local copies, waits for them, and re-layouts  3.37 us
  transfers between devices with their start and end apart: 22, of which 10 were waited for; matrix products, arithmetic and copies ran while one was open for 21% of the time, Pallas kernels for 0%

profile of v4, /device:TPU:0, one launch (start us, length us, event | category | flops | bytes accessed | tf_op | source)
XLA Modules:
  0.0 139.8 jit_solution(1004397646643381099)
XLA Ops:
  0.6 3.0 %collective-permute-start = (bf16[1,512,128]{2,1,0:T(8,128)(2,1)}, bf16[1,512,128]{2,1,0:T(8,128)(2,1)S(1)}, u32[]{:S(2)}, u32[]{:S(2)}) collective-permute-start(bf16[1,512,128]{2,1,0:T(8,128)(2,1)} %param.7), channel_id=1, source_target_pairs={{0,2},{1,3},{2,0},{3,1},{4,6},{5,7},{6,4},{7,5},{8,10},{9,11},{10,... | collective-permute-start | bytes 393224 | tf_op jit(solution)/shard_map/ppermute | solution.py:9
  3.7 1.6 %fusion.77 = (bf16[7,128,512]{2,1,0:T(8,128)(2,1)S(1)}, bf16[7,128,512]{2,1,0:T(8,128)(2,1)S(1)}) fusion(bf16[14,128,512]{2,1,0:T(8,128)(2,1)} %param.8), kind=kLoop, calls=%fused_computation.141 | loop fusion | bytes 3670016 | tf_op jit(solution)/shard_map/slice | solution.py:66
  5.4 2.6 %fusion.76 = (bf16[7,128,512]{2,1,0:T(8,128)(2,1)}, bf16[7,128,512]{2,1,0:T(8,128)(2,1)S(1)}) fusion(bf16[14,128,512]{2,1,0:T(8,128)(2,1)} %param.9), kind=kLoop, calls=%fused_computation.140 | loop fusion | bytes 3670016 | tf_op jit(solution)/shard_map/slice | solution.py:84
  9.3 1.6 %fusion.39 = f32[7,128,512]{2,1,0:T(8,128)} fusion(bf16[7,128,512]{2,1,0:T(8,128)(2,1)S(1)} %get-tuple-element.11, bf16[7,128,512]{2,1,0:T(8,128)(2,1)S(1)} %get-tuple-element.27, s32[]{:T(128)S(6)} %select_n.113), kind=kOutput, calls=%fused_computation.67 | convolution fusion | flops 117440512 | bytes 2981892 | tf_op jit(solution)/shard_map/lik,lkc->lic/dot_general | solution.py:61
  12.3 1.6 %collective-permute-start.5 = (bf16[129,512]{1,0:T(8,128)(2,1)S(1)}, bf16[129,512]{1,0:T(8,128)(2,1)S(1)}, u32[]{:S(2)}, u32[]{:S(2)}) collective-permute-start(bf16[129,512]{1,0:T(8,128)(2,1)S(1)} %get-tuple-element.35), channel_id=1, source_target_pairs={{0,4},{4,8},{8,12},{12,16},{16,20},{20,24},{24,28},{28,0},{1,5},{5... | collective-permute-start | bytes 396296 | tf_op jit(solution)/shard_map/ppermute | solution.py:23
  13.9 1.6 %collective-permute-start.6 = (bf16[129,512]{1,0:T(8,128)(2,1)S(1)}, bf16[129,512]{1,0:T(8,128)(2,1)S(1)}, u32[]{:S(2)}, u32[]{:S(2)}) collective-permute-start(bf16[129,512]{1,0:T(8,128)(2,1)S(1)} %get-tuple-element.35), channel_id=1, source_target_pairs={{0,8},{4,12},{8,16},{12,20},{16,24},{20,28},{24,0},{28,4},{1,9},{5... | collective-permute-start | bytes 396296 | tf_op jit(solution)/shard_map/ppermute | solution.py:23
  15.5 2.5 %collective-permute-start.7 = (bf16[129,512]{1,0:T(8,128)(2,1)S(1)}, bf16[129,512]{1,0:T(8,128)(2,1)S(1)}, u32[]{:S(2)}, u32[]{:S(2)}) collective-permute-start(bf16[129,512]{1,0:T(8,128)(2,1)S(1)} %get-tuple-element.35), channel_id=1, source_target_pairs={{0,12},{4,16},{8,20},{12,24},{16,28},{20,0},{24,4},{28,8},{1,13},{... | collective-permute-start | bytes 396296 | tf_op jit(solution)/shard_map/ppermute | solution.py:23
  19.2 11.8 %collective-permute-done.1 = bf16[7,128,512]{2,1,0:T(8,128)(2,1)} collective-permute-done((bf16[7,128,512]{2,1,0:T(8,128)(2,1)S(1)}, bf16[7,128,512]{2,1,0:T(8,128)(2,1)}, u32[]{:S(2)}, u32[]{:S(2)}) %collective-permute-start.1) | collective-permute-done | bytes 917536 | tf_op jit(solution)/shard_map/ppermute | solution.py:9
  31.0 3.5 %collective-permute-start.9 = (bf16[129,512]{1,0:T(8,128)(2,1)S(1)}, bf16[129,512]{1,0:T(8,128)(2,1)S(1)}, u32[]{:S(2)}, u32[]{:S(2)}) collective-permute-start(bf16[129,512]{1,0:T(8,128)(2,1)S(1)} %get-tuple-element.35), channel_id=1, source_target_pairs={{0,20},{4,24},{8,28},{12,0},{16,4},{20,8},{24,12},{28,16},{1,21},{... | collective-permute-start | bytes 396296 | tf_op jit(solution)/shard_map/ppermute | solution.py:23
  38.8 5.3 %collective-permute-done.10 = bf16[129,512]{1,0:T(8,128)(2,1)S(1)} collective-permute-done((bf16[129,512]{1,0:T(8,128)(2,1)S(1)}, bf16[129,512]{1,0:T(8,128)(2,1)S(1)}, u32[]{:S(2)}, u32[]{:S(2)}) %collective-permute-start.10) | collective-permute-done | bytes 132128 | tf_op jit(solution)/shard_map/ppermute | solution.py:23
  45.3 1.6 %fusion.36 = f32[7,128,512]{2,1,0:T(8,128)S(1)} fusion(bf16[7,128,512]{2,1,0:T(8,128)(2,1)} %collective-permute-done.1, bf16[7,128,512]{2,1,0:T(8,128)(2,1)S(1)} %copy-done.7, s32[]{:T(128)S(6)} %select_n.115), kind=kOutput, calls=%fused_computation.64 | convolution fusion | flops 117440512 | bytes 2981892 | tf_op jit(solution)/shard_map/lik,lkc->lic/dot_general | solution.py:61
  48.3 1.7 %fusion.79 = (bf16[7,128,512]{2,1,0:T(8,128)(2,1)S(1)}, f32[7,128,512]{2,1,0:T(8,128)}) fusion(bf16[2,7,128,512]{3,2,1,0:T(8,128)(2,1)S(1)} %collective-permute-done.2, bf16[7,128,512]{2,1,0:T(8,128)(2,1)S(1)} %copy-done.7, s32[]{:T(128)S(6)} %select_n.116, f32[7,128,512]{2,1,0:T(8,128)S(1)} %fusion.36, f32[7,128,512]{2,1,0:T(8,128)S(1)} %copy-done, ...), kind=kOutput, calls=%fused_computation.143 | convolution fusion | flops 119275520 | bytes 9404420 | tf_op jit(solution)/shard_map/lik,lkc->lic/dot_general | solution.py:61
  50.0 16.3 %collective-permute-done.3 = bf16[7,128,512]{2,1,0:T(8,128)(2,1)S(1)} collective-permute-done((bf16[7,128,512]{2,1,0:T(8,128)(2,1)S(1)}, bf16[7,128,512]{2,1,0:T(8,128)(2,1)S(1)}, u32[]{:S(2)}, u32[]{:S(2)}) %collective-permute-start.3) | collective-permute-done | bytes 917536 | tf_op jit(solution)/shard_map/ppermute | solution.py:9
  67.9 2.1 %fusion.44 = f32[14,1,128]{2,1,0:T(1,128)S(1)} fusion(bf16[14,128,512]{2,1,0:T(8,128)(2,1)} %param.10, bf16[14,512,1]{1,0,2:T(8,128)(2,1)S(1)} %bitcast.128), kind=kOutput, calls=%fused_computation.84 | convolution fusion | flops 1835008 | bytes 1856512 | tf_op jit(solution)/shard_map/lab,lb->la/dot_general | solution.py:115
  73.6 3.0 %fusion.80 = (bf16[7,128,512]{2,1,0:T(8,128)(2,1)S(1)}, f32[7,128,512]{2,1,0:T(8,128)}) fusion(bf16[2,7,128,512]{3,2,1,0:T(8,128)(2,1)} %collective-permute-done.12, bf16[7,128,512]{2,1,0:T(8,128)(2,1)S(1)} %copy-done.5, s32[]{:T(128)S(6)} %select_n.116, f32[7,128,512]{2,1,0:T(8,128)S(1)} %fusion.27, f32[7,128,512]{2,1,0:T(8,128)S(1)} %fusion.30, ...), kind=kOutput, calls=%fused_computation.144 | convolution fusion | flops 119275520 | bytes 9404420 | tf_op jit(solution)/shard_map/lik,lkc->lic/dot_general | solution.py:61
  76.6 16.7 %collective-permute-done.13 = bf16[7,128,512]{2,1,0:T(8,128)(2,1)S(1)} collective-permute-done((bf16[7,128,512]{2,1,0:T(8,128)(2,1)S(1)}, bf16[7,128,512]{2,1,0:T(8,128)(2,1)S(1)}, u32[]{:S(2)}, u32[]{:S(2)}) %collective-permute-start.13) | collective-permute-done | bytes 917536 | tf_op jit(solution)/shard_map/ppermute | solution.py:9
  94.8 2.0 %gather_fusion.1 = bf16[14,129,512]{2,1,0:T(8,128)(2,1)} fusion(bf16[8,129,512]{2,1,0:T(8,128)(2,1)S(1)} %bitcast_dynamic-update-slice_fusion, s32[1024]{0:T(1024)S(1)} %get-tuple-element.41), kind=kCustom, calls=%fused_computation.1 | custom fusion | bytes 3698744 | tf_op jit(solution)/shard_map/jit(_take)/gather | solution.py:91
  96.8 1.9 %broadcast_select_fusion = bf16[14,129,512]{2,1,0:T(8,128)(2,1)S(1)} fusion(bf16[14,129,512]{2,1,0:T(8,128)(2,1)} %gather_fusion.1, pred[14]{0:T(512)(128)(4,1)S(1)} %get-tuple-element.22), kind=kLoop, calls=%fused_computation.8 | loop fusion | flops 924672 | bytes 3698702 | tf_op jit(solution)/shard_map/jit(_take)/select_n | solution.py:91
  99.1 16.2 %collective-permute-done.15 = bf16[7,128,512]{2,1,0:T(8,128)(2,1)} collective-permute-done((bf16[7,128,512]{2,1,0:T(8,128)(2,1)S(1)}, bf16[7,128,512]{2,1,0:T(8,128)(2,1)}, u32[]{:S(2)}, u32[]{:S(2)}) %collective-permute-start.15) | collective-permute-done | bytes 917536 | tf_op jit(solution)/shard_map/ppermute | solution.py:9
  117.9 1.6 %fusion.18 = f32[7,128,512]{2,1,0:T(8,128)S(1)} fusion(bf16[7,128,512]{2,1,0:T(8,128)(2,1)} %collective-permute-done.15, bf16[7,128,512]{2,1,0:T(8,128)(2,1)S(1)} %get-tuple-element.25, s32[]{:T(128)S(6)} %select_n.115), kind=kOutput, calls=%fused_computation.46 | convolution fusion | flops 117440512 | bytes 2981892 | tf_op jit(solution)/shard_map/lik,lkc->lic/dot_general | solution.py:61
  124.5 1.8 %collective-permute-start.19 = (f32[4,128]{1,0:T(4,128)S(1)}, f32[4,128]{1,0:T(4,128)S(1)}, u32[]{:S(2)}, u32[]{:S(2)}) collective-permute-start(f32[4,128]{1,0:T(4,128)S(1)} %constant_dynamic-slice_fusion.4), channel_id=1, source_target_pairs={{0,16},{4,20},{8,24},{12,28},{16,0},{20,4},{24,8},{28,12},{1,17},{... | collective-permute-start | bytes 6152 | tf_op jit(solution)/shard_map/ppermute | solution.py:9
  126.3 2.7 %collective-permute-done.19 = f32[4,128]{1,0:T(4,128)S(1)} collective-permute-done((f32[4,128]{1,0:T(4,128)S(1)}, f32[4,128]{1,0:T(4,128)S(1)}, u32[]{:S(2)}, u32[]{:S(2)}) %collective-permute-start.19) | collective-permute-done | bytes 2080 | tf_op jit(solution)/shard_map/ppermute | solution.py:9
  129.0 3.8 %collective-permute-start.20 = (f32[2,128]{1,0:T(2,128)S(1)}, f32[2,128]{1,0:T(2,128)S(1)}, u32[]{:S(2)}, u32[]{:S(2)}) collective-permute-start(f32[2,128]{1,0:T(2,128)S(1)} %constant_dynamic-slice_fusion.2), channel_id=1, source_target_pairs={{0,8},{4,12},{8,0},{12,4},{16,24},{20,28},{24,16},{28,20},{1,9},{5... | collective-permute-start | bytes 3080 | tf_op jit(solution)/shard_map/ppermute | solution.py:9
  134.3 2.8 %collective-permute-start.21 = (f32[1,128]{1,0:T(1,128)S(1)}, f32[1,128]{1,0:T(1,128)S(1)}, u32[]{:S(2)}, u32[]{:S(2)}) collective-permute-start(f32[1,128]{1,0:T(1,128)S(1)} %constant_dynamic-slice_fusion), channel_id=1, source_target_pairs={{0,4},{4,0},{8,12},{12,8},{16,20},{20,16},{24,28},{28,24},{1,5},{5... | collective-permute-start | bytes 1544 | tf_op jit(solution)/shard_map/ppermute | solution.py:9
  (115 shorter events, 29.4 us)
Async XLA Ops:
  0.6 7.4 %collective-permute-start = (bf16[1,512,128]{2,1,0:T(8,128)(2,1)}, bf16[1,512,128]{2,1,0:T(8,128)(2,1)S(1)}, u32[]{:S(2)}, u32[]{:S(2)}) collective-permute-start(bf16[1,512,128]{2,1,0:T(8,128)(2,1)} %param.7), channel_id=1, source_target_pairs={{0,2},{1,3},{2,0},{3,1},{4,6},{5,7},{6,4},{7,5},{8,10},{9,11},{10,... | collective-permute-start | bytes 393224 | tf_op jit(solution)/shard_map/ppermute | solution.py:9
  8.1 2.8 %collective-permute-start.4 = (bf16[2,1,512,128]{3,2,1,0:T(8,128)(2,1)S(1)}, bf16[2,1,512,128]{3,2,1,0:T(8,128)(2,1)S(1)}, u32[]{:S(2)}, u32[]{:S(2)}) collective-permute-start(bf16[2,1,512,128]{3,2,1,0:T(8,128)(2,1)S(1)} %pad_maximum_fusion.5), channel_id=1, source_target_pairs={{0,1},{1,0},{2,3},{3,2},{4,5},{5,4},{6,7},{7,6},{8,9},{9,8},{10,11... | collective-permute-start | bytes 786440 | tf_op jit(solution)/shard_map/ppermute | solution.py:9
  8.2 22.9 %collective-permute-start.1 = (bf16[7,128,512]{2,1,0:T(8,128)(2,1)S(1)}, bf16[7,128,512]{2,1,0:T(8,128)(2,1)}, u32[]{:S(2)}, u32[]{:S(2)}) collective-permute-start(bf16[7,128,512]{2,1,0:T(8,128)(2,1)S(1)} %get-tuple-element.11), channel_id=1, source_target_pairs={{0,2},{1,3},{2,0},{3,1},{4,6},{5,7},{6,4},{7,5},{8,10},{9,11},{10,... | collective-permute-start | bytes 2752520 | tf_op jit(solution)/shard_map/ppermute | solution.py:9
  12.3 23.6 %collective-permute-start.5 = (bf16[129,512]{1,0:T(8,128)(2,1)S(1)}, bf16[129,512]{1,0:T(8,128)(2,1)S(1)}, u32[]{:S(2)}, u32[]{:S(2)}) collective-permute-start(bf16[129,512]{1,0:T(8,128)(2,1)S(1)} %get-tuple-element.35), channel_id=1, source_target_pairs={{0,4},{4,8},{8,12},{12,16},{16,20},{20,24},{24,28},{28,0},{1,5},{5... | collective-permute-start | bytes 396296 | tf_op jit(solution)/shard_map/ppermute | solution.py:23
  13.9 22.2 %collective-permute-start.6 = (bf16[129,512]{1,0:T(8,128)(2,1)S(1)}, bf16[129,512]{1,0:T(8,128)(2,1)S(1)}, u32[]{:S(2)}, u32[]{:S(2)}) collective-permute-start(bf16[129,512]{1,0:T(8,128)(2,1)S(1)} %get-tuple-element.35), channel_id=1, source_target_pairs={{0,8},{4,12},{8,16},{12,20},{16,24},{20,28},{24,0},{28,4},{1,9},{5... | collective-permute-start | bytes 396296 | tf_op jit(solution)/shard_map/ppermute | solution.py:23
  15.5 22.0 %collective-permute-start.7 = (bf16[129,512]{1,0:T(8,128)(2,1)S(1)}, bf16[129,512]{1,0:T(8,128)(2,1)S(1)}, u32[]{:S(2)}, u32[]{:S(2)}) collective-permute-start(bf16[129,512]{1,0:T(8,128)(2,1)S(1)} %get-tuple-element.35), channel_id=1, source_target_pairs={{0,12},{4,16},{8,20},{12,24},{16,28},{20,0},{24,4},{28,8},{1,13},{... | collective-permute-start | bytes 396296 | tf_op jit(solution)/shard_map/ppermute | solution.py:23
  18.0 20.1 %collective-permute-start.8 = (bf16[129,512]{1,0:T(8,128)(2,1)S(1)}, bf16[129,512]{1,0:T(8,128)(2,1)S(1)}, u32[]{:S(2)}, u32[]{:S(2)}) collective-permute-start(bf16[129,512]{1,0:T(8,128)(2,1)S(1)} %get-tuple-element.35), channel_id=1, source_target_pairs={{0,16},{4,20},{8,24},{12,28},{16,0},{20,4},{24,8},{28,12},{1,17},{... | collective-permute-start | bytes 396296 | tf_op jit(solution)/shard_map/ppermute | solution.py:23
  31.0 7.8 %collective-permute-start.9 = (bf16[129,512]{1,0:T(8,128)(2,1)S(1)}, bf16[129,512]{1,0:T(8,128)(2,1)S(1)}, u32[]{:S(2)}, u32[]{:S(2)}) collective-permute-start(bf16[129,512]{1,0:T(8,128)(2,1)S(1)} %get-tuple-element.35), channel_id=1, source_target_pairs={{0,20},{4,24},{8,28},{12,0},{16,4},{20,8},{24,12},{28,16},{1,21},{... | collective-permute-start | bytes 396296 | tf_op jit(solution)/shard_map/ppermute | solution.py:23
  35.9 9.3 %copy-start.7 = (bf16[7,128,512]{2,1,0:T(8,128)(2,1)S(1)}, bf16[7,128,512]{2,1,0:T(8,128)(2,1)}, u32[]{:S(2)}) copy-start(bf16[7,128,512]{2,1,0:T(8,128)(2,1)} %copy-done.6) | copy-start | bytes 2752516
  35.9 10.9 %collective-permute-start.2 = (bf16[2,7,128,512]{3,2,1,0:T(8,128)(2,1)S(1)}, bf16[2,7,128,512]{3,2,1,0:T(8,128)(2,1)S(1)}, u32[]{:S(2)}, u32[]{:S(2)}) collective-permute-start(bf16[2,7,128,512]{3,2,1,0:T(8,128)(2,1)S(1)} %pad_maximum_fusion.1), channel_id=1, source_target_pairs={{0,1},{1,0},{2,3},{3,2},{4,5},{5,4},{6,7},{7,6},{8,9},{9,8},{10,11... | collective-permute-start | bytes 5505032 | tf_op jit(solution)/shard_map/ppermute | solution.py:9
  36.0 8.0 %collective-permute-start.10 = (bf16[129,512]{1,0:T(8,128)(2,1)S(1)}, bf16[129,512]{1,0:T(8,128)(2,1)S(1)}, u32[]{:S(2)}, u32[]{:S(2)}) collective-permute-start(bf16[129,512]{1,0:T(8,128)(2,1)S(1)} %get-tuple-element.35), channel_id=1, source_target_pairs={{0,24},{4,28},{8,0},{12,4},{16,8},{20,12},{24,16},{28,20},{1,25},{... | collective-permute-start | bytes 396296 | tf_op jit(solution)/shard_map/ppermute | solution.py:23
  37.5 6.6 %collective-permute-start.11 = (bf16[129,512]{1,0:T(8,128)(2,1)S(1)}, bf16[129,512]{1,0:T(8,128)(2,1)S(1)}, u32[]{:S(2)}, u32[]{:S(2)}) collective-permute-start(bf16[129,512]{1,0:T(8,128)(2,1)S(1)} %get-tuple-element.35), channel_id=1, source_target_pairs={{0,28},{4,0},{8,4},{12,8},{16,12},{20,16},{24,20},{28,24},{1,29},{... | collective-permute-start | bytes 396296 | tf_op jit(solution)/shard_map/ppermute | solution.py:23
  44.1 22.2 %collective-permute-start.3 = (bf16[7,128,512]{2,1,0:T(8,128)(2,1)S(1)}, bf16[7,128,512]{2,1,0:T(8,128)(2,1)S(1)}, u32[]{:S(2)}, u32[]{:S(2)}) collective-permute-start(bf16[7,128,512]{2,1,0:T(8,128)(2,1)S(1)} %get-tuple-element.13), channel_id=1, source_target_pairs={{0,2},{1,3},{2,0},{3,1},{4,6},{5,7},{6,4},{7,5},{8,10},{9,11},{10,... | collective-permute-start | bytes 2752520 | tf_op jit(solution)/shard_map/ppermute | solution.py:9
  67.9 4.1 %collective-permute-start.12 = (bf16[2,7,128,512]{3,2,1,0:T(8,128)(2,1)}, bf16[2,7,128,512]{3,2,1,0:T(8,128)(2,1)}, u32[]{:S(2)}, u32[]{:S(2)}) collective-permute-start(bf16[2,7,128,512]{3,2,1,0:T(8,128)(2,1)} %pad_maximum_fusion.2), channel_id=1, source_target_pairs={{0,1},{1,0},{2,3},{3,2},{4,5},{5,4},{6,7},{7,6},{8,9},{9,8},{10,11... | collective-permute-start | bytes 5505032 | tf_op jit(solution)/shard_map/ppermute | solution.py:9
  70.4 22.8 %collective-permute-start.13 = (bf16[7,128,512]{2,1,0:T(8,128)(2,1)S(1)}, bf16[7,128,512]{2,1,0:T(8,128)(2,1)S(1)}, u32[]{:S(2)}, u32[]{:S(2)}) collective-permute-start(bf16[7,128,512]{2,1,0:T(8,128)(2,1)S(1)} %get-tuple-element.16), channel_id=1, source_target_pairs={{0,2},{1,3},{2,0},{3,1},{4,6},{5,7},{6,4},{7,5},{8,10},{9,11},{10,... | collective-permute-start | bytes 2752520 | tf_op jit(solution)/shard_map/ppermute | solution.py:9
  73.6 20.8 %copy-start.1 = (bf16[14,128,512]{2,1,0:T(8,128)(2,1)S(1)}, bf16[14,128,512]{2,1,0:T(8,128)(2,1)}, u32[]{:S(2)}) copy-start(bf16[14,128,512]{2,1,0:T(8,128)(2,1)} %param.8) | copy-start | bytes 5505028
  93.3 22.0 %collective-permute-start.15 = (bf16[7,128,512]{2,1,0:T(8,128)(2,1)S(1)}, bf16[7,128,512]{2,1,0:T(8,128)(2,1)}, u32[]{:S(2)}, u32[]{:S(2)}) collective-permute-start(bf16[7,128,512]{2,1,0:T(8,128)(2,1)S(1)} %get-tuple-element.19), channel_id=1, source_target_pairs={{0,2},{1,3},{2,0},{3,1},{4,6},{5,7},{6,4},{7,5},{8,10},{9,11},{10,... | collective-permute-start | bytes 2752520 | tf_op jit(solution)/shard_map/ppermute | solution.py:9
  98.8 20.7 %collective-permute-start.14 = (bf16[2,7,128,512]{3,2,1,0:T(8,128)(2,1)S(1)}, bf16[2,7,128,512]{3,2,1,0:T(8,128)(2,1)S(1)}, u32[]{:S(2)}, u32[]{:S(2)}) collective-permute-start(bf16[2,7,128,512]{3,2,1,0:T(8,128)(2,1)S(1)} %pad_maximum_fusion.3), channel_id=1, source_target_pairs={{0,1},{1,0},{2,3},{3,2},{4,5},{5,4},{6,7},{7,6},{8,9},{9,8},{10,11... | collective-permute-start | bytes 5505032 | tf_op jit(solution)/shard_map/ppermute | solution.py:9
  116.6 3.9 %collective-permute-start.16 = (bf16[2,7,128,512]{3,2,1,0:T(8,128)(2,1)S(1)}, bf16[2,7,128,512]{3,2,1,0:T(8,128)(2,1)S(1)}, u32[]{:S(2)}, u32[]{:S(2)}) collective-permute-start(bf16[2,7,128,512]{3,2,1,0:T(8,128)(2,1)S(1)} %pad_maximum_fusion.4), channel_id=1, source_target_pairs={{0,1},{1,0},{2,3},{3,2},{4,5},{5,4},{6,7},{7,6},{8,9},{9,8},{10,11... | collective-permute-start | bytes 5505032 | tf_op jit(solution)/shard_map/ppermute | solution.py:9
  124.5 4.5 %collective-permute-start.19 = (f32[4,128]{1,0:T(4,128)S(1)}, f32[4,128]{1,0:T(4,128)S(1)}, u32[]{:S(2)}, u32[]{:S(2)}) collective-permute-start(f32[4,128]{1,0:T(4,128)S(1)} %constant_dynamic-slice_fusion.4), channel_id=1, source_target_pairs={{0,16},{4,20},{8,24},{12,28},{16,0},{20,4},{24,8},{28,12},{1,17},{... | collective-permute-start | bytes 6152 | tf_op jit(solution)/shard_map/ppermute | solution.py:9
  129.0 5.3 %collective-permute-start.20 = (f32[2,128]{1,0:T(2,128)S(1)}, f32[2,128]{1,0:T(2,128)S(1)}, u32[]{:S(2)}, u32[]{:S(2)}) collective-permute-start(f32[2,128]{1,0:T(2,128)S(1)} %constant_dynamic-slice_fusion.2), channel_id=1, source_target_pairs={{0,8},{4,12},{8,0},{12,4},{16,24},{20,28},{24,16},{28,20},{1,9},{5... | collective-permute-start | bytes 3080 | tf_op jit(solution)/shard_map/ppermute | solution.py:9
  132.8 4.4 %collective-permute-start.17 = (f32[14,256]{1,0:T(8,128)S(1)}, f32[14,256]{1,0:T(8,128)S(1)}, u32[]{:S(2)}, u32[]{:S(2)}) collective-permute-start(f32[14,256]{1,0:T(8,128)S(1)} %constant_dynamic-slice_fusion.8), channel_id=1, source_target_pairs={{0,2},{1,3},{2,0},{3,1},{4,6},{5,7},{6,4},{7,5},{8,10},{9,11},{10,... | collective-permute-start | bytes 43016 | tf_op jit(solution)/shard_map/ppermute | solution.py:9
  134.3 4.3 %collective-permute-start.21 = (f32[1,128]{1,0:T(1,128)S(1)}, f32[1,128]{1,0:T(1,128)S(1)}, u32[]{:S(2)}, u32[]{:S(2)}) collective-permute-start(f32[1,128]{1,0:T(1,128)S(1)} %constant_dynamic-slice_fusion), channel_id=1, source_target_pairs={{0,4},{4,0},{8,12},{12,8},{16,20},{20,16},{24,28},{28,24},{1,5},{5... | collective-permute-start | bytes 1544 | tf_op jit(solution)/shard_map/ppermute | solution.py:9
  137.1 2.0 %collective-permute-start.18 = (f32[14,128]{1,0:T(8,128)S(1)}, f32[14,128]{1,0:T(8,128)S(1)}, u32[]{:S(2)}, u32[]{:S(2)}) collective-permute-start(f32[14,128]{1,0:T(8,128)S(1)} %constant_dynamic-slice_fusion.7), channel_id=1, source_target_pairs={{0,1},{1,0},{2,3},{3,2},{4,5},{5,4},{6,7},{7,6},{8,9},{9,8},{10,11... | collective-permute-start | bytes 21512 | tf_op jit(solution)/shard_map/ppermute | solution.py:9
  (14 other events, 27.7 us)
